TPU v7x, 128 devices: a whole 4x4x4 slice. The times are simulated.
128 devices in a mesh: dp: 16 (over x, y_lo, core), ctx: 8 (over z, y_hi).
Axes of the slice: x: 4, y: 4 (y_hi: 2, y_lo: 2; y = y_hi * 2 + y_lo), z: 4, core: 2. Of those that a mesh axis runs over, the one named last changes fastest.
Arguments:
- ids: int32 [2048], P('ctx'), may hold values from 0 to 511
- tags: int32 [2048], P('ctx'), may hold values from 0 to 3
- embed: bfloat16 [512, 4096], P(None, 'dp'), may hold values from -21 to 21
- gain: float32 [4096], P('dp'), may hold values from 0.5 to 1.5
- w_in: bfloat16 [3, 4096, 4096], P(None, None, 'dp'), may hold values from -0.125 to 0.125
- short_filt: float32 [3, 7, 4096], P(None, None, 'dp'), may hold values from -2.4 to 2.4
- mr_filt: float32 [128, 4096], P(None, 'dp'), may hold values from -0.9 to 0.9
- rates: float32 [4096], P('dp'), may hold values from 0.004 to 0.12
- w_out: bfloat16 [4096, 4096], P('dp'), may hold values from -0.125 to 0.125
- w_tag: bfloat16 [4096, 4], P('dp'), may hold values from -0.25 to 0.25
Outputs:
- loss: float32 [], replicated
- block_out: bfloat16 [2048, 4096], P('ctx', 'dp')
- d_embed: float32 [512, 4096], P('ctx', 'dp')
- d_gain: float32 [4096], P('dp')
- d_w_in: float32 [3, 4096, 4096], P(None, 'ctx', 'dp')
- d_short: float32 [3, 7, 4096], P(None, None, 'dp')
- d_mr: float32 [128, 4096], P(None, 'dp')
- d_rates: float32 [4096], P('dp')
- d_w_out: float32 [4096, 4096], P('dp', 'ctx')
- d_w_tag: float32 [4096, 4], P('dp')
All inputs are finite; a program needn't handle non-finite values.
Results may differ from a plain program's by a relative error of at most 0.025.
Values may be sent and summed in bfloat16 or wider, within the bound.
No kernel may reach another device: no remote copies, remote signals or barrier semaphores. Data moves between devices by JAX's collectives and lax.ppermute only.
A program may use at most 128 MiB of HBM per device.

v0:
```python
import jax
import jax.numpy as jnp
from jax import lax
from jax.sharding import PartitionSpec as P
from jax.experimental import pallas as pl

LANES = 128
ROW_BLOCK = 64


def medium_forward(kv_ext, taps_eff, rows):
    span, width = taps_eff.shape

    def kernel(kv_ref, g_ref, m_ref):
        for rb in range(0, rows, ROW_BLOCK):

            def step(s, acc):
                start = span - 1 - s + rb
                return acc + g_ref[pl.ds(s, 1), :] * kv_ref[pl.ds(start, ROW_BLOCK), :]

            acc = lax.fori_loop(
                0, span, step, jnp.zeros((ROW_BLOCK, LANES), jnp.float32), unroll=8
            )
            m_ref[rb : rb + ROW_BLOCK, :] = acc

    ext = kv_ext.shape[0]
    return pl.pallas_call(
        kernel,
        out_shape=jax.ShapeDtypeStruct((rows, width), jnp.float32),
        grid=(width // LANES,),
        in_specs=[
            pl.BlockSpec((ext, LANES), lambda c: (0, c)),
            pl.BlockSpec((span, LANES), lambda c: (0, c)),
        ],
        out_specs=pl.BlockSpec((rows, LANES), lambda c: (0, c)),
    )(kv_ext, taps_eff)


def medium_backward(dm_ext, kv_ext, taps_eff, rows):
    span, width = taps_eff.shape

    def kernel(dm_ref, kv_ref, g_ref, dkv_ref, corr_ref):
        for rb in range(0, rows, ROW_BLOCK):

            def step(s, acc):
                return acc + g_ref[pl.ds(s, 1), :] * dm_ref[pl.ds(s + rb, ROW_BLOCK), :]

            acc = lax.fori_loop(
                0, span, step, jnp.zeros((ROW_BLOCK, LANES), jnp.float32), unroll=8
            )
            dkv_ref[rb : rb + ROW_BLOCK, :] = acc

        def lag_group(g, carry):
            s0 = pl.multiple_of(g * 8, 8)
            parts = []
            for i in range(8):
                start = span - 1 - s0 - i
                part = jnp.zeros((8, LANES), jnp.float32)
                for rb in range(0, rows, 8):
                    part = part + dm_ref[rb : rb + 8, :] * kv_ref[pl.ds(start + rb, 8), :]
                parts.append(jnp.sum(part, axis=0, keepdims=True))
            corr_ref[pl.ds(s0, 8), :] = jnp.concatenate(parts, axis=0)
            return carry

        lax.fori_loop(0, span // 8, lag_group, 0)

    ext = kv_ext.shape[0]
    return pl.pallas_call(
        kernel,
        out_shape=(
            jax.ShapeDtypeStruct((rows, width), jnp.float32),
            jax.ShapeDtypeStruct((span, width), jnp.float32),
        ),
        grid=(width // LANES,),
        in_specs=[
            pl.BlockSpec((dm_ext.shape[0], LANES), lambda c: (0, c)),
            pl.BlockSpec((ext, LANES), lambda c: (0, c)),
            pl.BlockSpec((span, LANES), lambda c: (0, c)),
        ],
        out_specs=(
            pl.BlockSpec((rows, LANES), lambda c: (0, c)),
            pl.BlockSpec((span, LANES), lambda c: (0, c)),
        ),
    )(dm_ext, kv_ext, taps_eff)


def shifted(block, axis, distance):
    devices = range(lax.axis_size(axis))
    route = [(i - distance, i) for i in devices if i - distance in devices]
    return lax.ppermute(block, axis, route)


def short_filter(padded, filters, count):
    taps = filters.shape[1]
    total = jnp.zeros((count,) + padded.shape[1:], jnp.float32)
    for s in range(taps):
        total = total + filters[None, :, s, :] * padded[taps - 1 - s : taps - 1 - s + count].astype(
            jnp.float32
        )
    return total


def split3(x):
    parts = []
    rest = x
    for _ in range(3):
        part = lax.reduce_precision(rest, exponent_bits=8, mantissa_bits=7)
        parts.append(part)
        rest = rest - part
    return [p.astype(jnp.bfloat16) for p in parts]


def split2(x):
    hi = lax.reduce_precision(x, exponent_bits=8, mantissa_bits=7)
    return [hi.astype(jnp.bfloat16), (x - hi).astype(jnp.bfloat16)]


def as_rows(flat, width):
    pad = (-flat.shape[0]) % width
    return jnp.pad(flat, (0, pad)).reshape(-1, width)


def block(ids, tags, embed, gain, w_in, short_filt, mr_filt, rates, w_out, w_tag):
    f32 = jnp.float32
    bf16 = jnp.bfloat16
    high = lax.Precision.HIGHEST
    rows = ids.shape[0]
    vocab = embed.shape[0]
    cw = embed.shape[1]
    width = w_in.shape[1]
    taps = short_filt.shape[1]
    span = mr_filt.shape[0]
    n_tags = w_tag.shape[1]
    n_ctx = lax.axis_size("ctx")
    k_ctx = lax.axis_index("ctx")
    seq = rows * n_ctx

    n_dp = lax.axis_size("dp")
    half = vocab // 2
    packed = jnp.concatenate([embed[:half], jnp.stack(split3(gain), axis=0), w_tag.T], axis=0)
    packed_full = lax.all_gather(packed, "dp", axis=1, tiled=True)
    upper = lax.all_to_all(
        jnp.broadcast_to(embed[None, half:], (n_dp, vocab - half, cw)), "dp", 0, 0, tiled=True
    )
    upper_full = jnp.transpose(upper, (1, 0, 2)).reshape(vocab - half, width)
    w_out_later, upper_full = lax.optimization_barrier((w_out, upper_full))
    w_out_cols = lax.all_to_all(w_out_later, "dp", 1, 0, tiled=True)
    embed_full = jnp.concatenate([packed_full[:half], upper_full], axis=0)
    gain_full = (
        packed_full[half].astype(f32) + packed_full[half + 1].astype(f32)
    ) + packed_full[half + 2].astype(f32)
    w_tag_full_t = packed_full[half + 3 : half + 3 + n_tags].astype(f32)

    emb32 = embed_full.astype(f32)
    r_vocab = lax.rsqrt(jnp.sum(emb32 * emb32, axis=1) / width + 1e-06)
    vocab_ids = jnp.arange(vocab)
    id_mask = ids[:, None] == vocab_ids[None, :]
    id_hot = id_mask.astype(bf16)
    r = jnp.sum(jnp.where(id_mask, r_vocab[None, :], 0.0), axis=1)[:, None]
    x0_full = jnp.dot(id_hot, embed_full, preferred_element_type=f32)
    x0 = jnp.dot(id_hot, embed, preferred_element_type=f32)
    u = (x0_full * r * gain_full[None, :]).astype(bf16)
    proj = jnp.einsum("td,jdc->tjc", u, w_in, preferred_element_type=f32).astype(bf16)
    head = shifted(proj[rows - (taps - 1) :], "ctx", 1)
    p_ext = jnp.concatenate([head, proj], axis=0)
    z = short_filter(p_ext, short_filt, rows)
    kv = (z[:, 1] * z[:, 2]).astype(bf16)
    kv_head = shifted(kv[rows - (span - 1) :], "ctx", 1)
    kv_ext = jnp.concatenate([kv_head, kv, jnp.zeros((1,) + kv.shape[1:], kv.dtype)], axis=0)
    q = z[:, 0]
    k = z[:, 1]
    v = z[:, 2]
    lags = jnp.arange(span).astype(f32)[:, None]
    decay = jnp.exp(-rates[None, :] * lags)
    taps_eff = mr_filt * decay
    kv_wide = kv_ext.astype(f32)
    m = medium_forward(kv_wide, taps_eff, rows)
    h = (q * m).astype(bf16)
    h_full = lax.all_gather(h, "dp", axis=1, tiled=True)
    y = jnp.dot(h_full, w_out_cols, preferred_element_type=f32)
    block_out = (x0 + y).astype(bf16)
    id_hi = (ids // 32).astype(bf16)
    id_lo = (ids % 32).astype(bf16)
    h_ids = jnp.concatenate([h, as_rows(jnp.concatenate([id_hi, id_lo]), cw)], axis=0)
    h_ids_all = lax.all_to_all(
        jnp.broadcast_to(h_ids[None], (n_ctx,) + h_ids.shape), "ctx", 0, 0, tiled=True
    )
    logit_part = jnp.dot(block_out, w_tag, preferred_element_type=f32)
    logit_parts = lax.all_to_all(
        jnp.broadcast_to(logit_part[None], (n_dp,) + logit_part.shape), "dp", 0, 0, tiled=True
    )
    logits = jnp.sum(logit_parts, axis=0)
    top = jnp.max(logits, axis=1)
    lse = top + jnp.log(jnp.sum(jnp.exp(logits - top[:, None]), axis=1))
    tag_hot = (tags[:, None] == jnp.arange(n_tags)[None, :]).astype(f32)
    loss_part = jnp.sum(lse - jnp.sum(logits * tag_hot, axis=1))
    dlog = jnp.exp(logits - lse[:, None]) - tag_hot
    dout = jnp.dot(dlog, w_tag.astype(f32).T, precision=high)
    tag_part = jnp.dot(block_out.astype(f32).T, dlog, precision=high)
    dy_full = jnp.dot(dlog, w_tag_full_t, precision=high).astype(bf16)
    dh = lax.dot_general(dy_full, w_out, (((1,), (1,)), ((), ())), preferred_element_type=f32)
    dq = dh * m
    dm = dh * q
    dm_tail = shifted(dm[: span - 1].astype(bf16), "ctx", -1).astype(f32)
    dm_ext = jnp.concatenate([dm, dm_tail, jnp.zeros((1,) + dm.shape[1:], f32)], axis=0)
    dkv, corr = medium_backward(dm_ext, kv_wide, taps_eff, rows)
    mr_part = corr * decay
    rate_part = -jnp.sum(lags * mr_filt * mr_part, axis=0)
    dz = jnp.stack([dq, dkv * v, dkv * k], axis=1)
    dz_tail = shifted(dz[: taps - 1], "ctx", -1)
    dz_ext = jnp.concatenate([dz, dz_tail], axis=0)
    dp = jnp.zeros_like(dz)
    shorts = []
    for s in range(taps):
        dp = dp + short_filt[None, :, s, :] * dz_ext[s : s + rows]
        shorts.append(jnp.sum(dz * p_ext[taps - 1 - s : taps - 1 - s + rows].astype(f32), axis=0))
    short_part = jnp.stack(shorts, axis=1)
    dpb = dp.astype(bf16)
    dp_all = lax.all_gather(jnp.transpose(dpb, (1, 0, 2)), "ctx", axis=1, tiled=True)
    du_part = jnp.einsum("tjc,jdc->td", dpb, w_in, preferred_element_type=f32)
    du_part, h_ids_all = lax.optimization_barrier((du_part, h_ids_all))
    dot_part = jnp.sum(du_part * gain_full[None, :] * x0_full, axis=1)
    dot_rows = as_rows(jnp.concatenate(split2(dot_part)), cw)
    n_dot = dot_rows.shape[0]
    du_send = jnp.concatenate(
        [
            du_part.astype(bf16).reshape(rows, n_dp, cw),
            jnp.broadcast_to(dot_rows[:, None, :], (n_dot, n_dp, cw)),
        ],
        axis=0,
    )
    du_recv = lax.all_to_all(du_send, "dp", 1, 1, tiled=True).astype(f32)
    du = jnp.sum(du_recv[:rows], axis=1)
    dot_recv = jnp.sum(du_recv[rows:], axis=1).reshape(-1)
    row_dot = (dot_recv[:rows] + dot_recv[rows : 2 * rows])[:, None] / width
    gain_part = jnp.sum(du * x0 * r, axis=0)
    dn = du * gain[None, :]
    dx0 = dout + r * (dn - x0 * r * r * row_dot)

    small = jnp.concatenate(
        [
            gain_part,
            short_part.reshape(-1),
            mr_part.reshape(-1),
            rate_part,
            tag_part.reshape(-1),
            loss_part[None],
        ]
    )
    n_small = small.shape[0]
    dlog_parts = split2(dlog.reshape(-1))
    tail = jnp.concatenate([small.astype(bf16)] + dlog_parts)
    final = jnp.concatenate(
        [dx0.astype(bf16), as_rows(tail, cw)],
        axis=0,
    )
    final_all = lax.all_to_all(
        jnp.broadcast_to(final[None], (n_ctx,) + final.shape), "ctx", 0, 0, tiled=True
    )
    dx0_all = final_all[:, :rows].reshape(seq, cw).astype(f32)
    tail_all = final_all[:, rows:].reshape(n_ctx, -1).astype(f32)
    small_tot = jnp.sum(tail_all[:, :n_small], axis=0)
    n_dlog = rows * n_tags
    dlog_all = (
        tail_all[:, n_small : n_small + n_dlog] + tail_all[:, n_small + n_dlog : n_small + 2 * n_dlog]
    ).reshape(seq, n_tags)

    h_all = h_ids_all[:, :rows].reshape(seq, cw)
    id_rows = h_ids_all[:, rows:].reshape(n_ctx, -1).astype(jnp.int32)
    ids_all = (id_rows[:, :rows] * 32 + id_rows[:, rows : 2 * rows]).reshape(seq)

    f_cols = width // n_ctx
    w_tag_cols = lax.dynamic_slice_in_dim(w_tag_full_t, k_ctx * f_cols, f_cols, 1)
    dy_all = jnp.dot(dlog_all, w_tag_cols, precision=high).astype(bf16)
    d_w_out = lax.dot_general(h_all, dy_all, (((0,), (0,)), ((), ())), preferred_element_type=f32)

    all_mask = ids_all[:, None] == vocab_ids[None, :]
    all_hot = all_mask.astype(bf16)
    r_all = jnp.sum(jnp.where(all_mask, r_vocab[None, :], 0.0), axis=1)[:, None]
    embed_k = lax.dynamic_slice_in_dim(embed_full, k_ctx * f_cols, f_cols, 1)
    gain_k = lax.dynamic_slice_in_dim(gain_full, k_ctx * f_cols, f_cols, 0)
    x0_k = jnp.dot(all_hot, embed_k, preferred_element_type=f32)
    u_k = (x0_k * r_all * gain_k[None, :]).astype(bf16)
    d_w_in = jnp.einsum("td,jtc->jdc", u_k, dp_all, preferred_element_type=f32)

    v_rows = vocab // n_ctx
    own_hot = (ids_all[:, None] == (k_ctx * v_rows + jnp.arange(v_rows))[None, :]).astype(f32)
    d_embed = jnp.dot(own_hot.T, dx0_all, precision=high)

    pos = 0
    outs = []
    for size, shape in (
        (cw, (cw,)),
        (3 * taps * cw, (3, taps, cw)),
        (span * cw, (span, cw)),
        (cw, (cw,)),
        (cw * n_tags, (cw, n_tags)),
        (1, ()),
    ):
        outs.append(small_tot[pos : pos + size].reshape(shape))
        pos += size
    gain_tot, short_tot, mr_tot, rate_tot, tag_tot, loss_tot = outs
    loss = loss_tot / seq
    return (
        loss,
        block_out,
        d_embed,
        gain_tot,
        d_w_in,
        short_tot,
        mr_tot,
        rate_tot,
        d_w_out,
        tag_tot,
    )


def solution(mesh):
    placed = (
        P("ctx"),
        P("ctx"),
        P(None, "dp"),
        P("dp"),
        P(None, None, "dp"),
        P(None, None, "dp"),
        P(None, "dp"),
        P("dp"),
        P("dp", None),
        P("dp", None),
    )
    return jax.shard_map(
        block,
        mesh=mesh,
        in_specs=placed,
        out_specs=(
            P(),
            P("ctx", "dp"),
            P("ctx", "dp"),
            P("dp"),
            P(None, "ctx", "dp"),
            P(None, None, "dp"),
            P(None, "dp"),
            P("dp"),
            P("dp", "ctx"),
            P("dp", None),
        ),
        check_vma=False,
    )
```

profile of v0, /device:TPU:0, one launch (start us, length us, event | category | flops | bytes accessed | tf_op | source)
XLA Modules:
  0.0 350.1 jit_solution(3936688235585524578)
XLA Ops:
  9.0 1.0 fusion.72
  11.0 1.5 broadcast_in_dim.39
  12.5 5.7 %all-to-all-start = ((bf16[16,256,256]{2,1,0:T(8,128)(2,1)}), bf16[16,256,256]{2,1,0:T(8,128)(2,1)}, u32[]{:S(2)}, u32[]{:S(2)}) async-start(bf16[16,256,256]{2,1,0:T(8,128)(2,1)} %broadcast_in_dim.39), calls=%async_computation | async-start | bytes 4194304 | tf_op jit(solution)/shard_map/all_to_all | solution.py:142
  18.4 31.1 %all-to-all-done = bf16[16,256,256]{2,1,0:T(8,128)(2,1)} async-done(((bf16[16,256,256]{2,1,0:T(8,128)(2,1)}), bf16[16,256,256]{2,1,0:T(8,128)(2,1)}, u32[]{:S(2)}, u32[]{:S(2)}) %all-to-all-start) | async-done | bytes 2097184 | tf_op jit(solution)/shard_map/all_to_all | solution.py:142
  49.6 2.9 copy.94
  52.4 14.9 %all-gather.4.cloned.1.call-done = bf16[263,4096]{0,1:T(8,128)(2,1)} async-done(((bf16[263,256]{0,1:T(8,128)(2,1)}), bf16[263,4096]{0,1:T(8,128)(2,1)}) %all-gather.4.cloned.1.call-update) | async-done | bytes 2154512 | tf_op jit(solution)/shard_map/all_gather | solution.py:141
  67.3 1.7 slice.226
  69.1 1.0 multiply_reduce_fusion
  70.2 4.3 %fusion.2 = f32[256,4096]{1,0:T(8,128)S(1)} fusion(bf16[256,4096]{0,1:T(8,128)(2,1)} %bitcast.121, bf16[256,4096]{0,1:T(8,128)(2,1)S(1)} %slice.226, s32[256]{0:T(256)S(1)} %copy-done.48), kind=kOutput, calls=%fused_computation.15 | convolution fusion | flops 1082261504 | bytes 8389632 | tf_op jit(solution)/shard_map/dot_general | solution.py:160
  74.7 2.5 fusion.70
  77.3 1.9 fusion.9
  79.2 4.8 %collective-permute-start = (bf16[6,3,256]{2,0,1:T(8,128)(2,1)S(1)}, bf16[6,3,256]{2,0,1:T(8,128)(2,1)S(1)}, u32[]{:S(2)}, u32[]{:S(2)}) collective-permute-start(bf16[6,3,256]{2,0,1:T(8,128)(2,1)S(1)} %slice.230), channel_id=1, source_target_pairs={{0,1},{1,2},{2,3},{3,4},{4,5},{5,6},{6,7},{8,9},{9,10},{10,11},{11... | collective-permute-start | bytes 27656 | tf_op jit(solution)/shard_map/ppermute | solution.py:90
  84.1 1.3 collective-permute-done
  86.1 0.9 copy-done.6
  87.1 5.7 %collective-permute-start.1 = (bf16[127,256]{1,0:T(8,128)(2,1)S(1)}, bf16[127,256]{1,0:T(8,128)(2,1)S(1)}, u32[]{:S(2)}, u32[]{:S(2)}) collective-permute-start(bf16[127,256]{1,0:T(8,128)(2,1)S(1)} %slice.244), channel_id=1, source_target_pairs={{0,1},{1,2},{2,3},{3,4},{4,5},{5,6},{6,7},{8,9},{9,10},{10,11},{11... | collective-permute-start | bytes 195080 | tf_op jit(solution)/shard_map/ppermute | solution.py:90
  93.6 1.0 collective-permute-done.1
  94.7 0.9 maximum_convert_fusion.kv_ref
  95.5 4.4 %shard_map.177 = f32[256,256]{1,0:T(8,128)} custom-call(f32[384,256]{1,0:T(8,128)} %maximum_convert_fusion.kv_ref, f32[128,256]{1,0:T(8,128)} %fusion.52.g_ref), custom_call_target="tpu_custom_call" | custom-call | tf_op jit(solution)/shard_map/pallas_call | solution.py:27
  99.9 1.7 multiply_convert_fusion.2
  101.7 4.1 %copy.95 = bf16[256,4096]{0,1:T(8,128)(2,1)} copy(bf16[256,4096]{1,0:T(8,128)(2,1)} %param.18) | data formatting | bytes 4194304 | tf_op jit(solution)/shard_map/optimization_barrier | solution.py:146
  105.7 4.5 %all-to-all-start.1 = ((bf16[256,16,256]{0,2,1:T(8,128)(2,1)}), bf16[256,16,256]{0,2,1:T(8,128)(2,1)}, u32[]{:S(2)}, u32[]{:S(2)}) async-start(bf16[256,16,256]{0,2,1:T(8,128)(2,1)} %bitcast.123), calls=%async_computation.1 | async-start | bytes 4194304 | tf_op jit(solution)/shard_map/all_to_all | solution.py:147
  111.5 1.2 fusion.40
  112.7 26.0 %all-to-all-done.1 = bf16[256,16,256]{0,2,1:T(8,128)(2,1)} async-done(((bf16[256,16,256]{0,2,1:T(8,128)(2,1)}), bf16[256,16,256]{0,2,1:T(8,128)(2,1)}, u32[]{:S(2)}, u32[]{:S(2)}) %all-to-all-start.1) | async-done | bytes 2097184 | tf_op jit(solution)/shard_map/all_to_all | solution.py:147
  138.7 3.9 %copy.96 = bf16[16,256,256]{2,1,0:T(8,128)(2,1)} copy(bf16[16,256,256]{1,2,0:T(8,128)(2,1)} %bitcast.8) | data formatting | bytes 4194304 | tf_op jit(solution)/shard_map/all_to_all | solution.py:147
  142.6 15.1 %all-gather.6.cloned.1.call-done = bf16[256,4096]{1,0:T(8,128)(2,1)} async-done(((bf16[256,256]{1,0:T(8,128)(2,1)}), bf16[256,4096]{1,0:T(8,128)(2,1)}) %all-gather.6.cloned.1.call-update) | async-done | bytes 2097168 | tf_op jit(solution)/shard_map/all_gather | solution.py:179
  157.7 3.0 fusion.12
  162.0 3.5 %all-to-all-start.2 = ((f32[16,256,4]{1,2,0:T(4,128)}), f32[16,256,4]{1,2,0:T(4,128)S(1)}, u32[]{:S(2)}, u32[]{:S(2)}) async-start(f32[16,256,4]{1,2,0:T(4,128)} %broadcast_in_dim.43), calls=%async_computation.2 | async-start | bytes 131072 | tf_op jit(solution)/shard_map/all_to_all | solution.py:189
  166.2 5.5 %all-to-all-done.2 = f32[16,256,4]{1,2,0:T(4,128)S(1)} async-done(((f32[16,256,4]{1,2,0:T(4,128)}), f32[16,256,4]{1,2,0:T(4,128)S(1)}, u32[]{:S(2)}, u32[]{:S(2)}) %all-to-all-start.2) | async-done | bytes 65568 | tf_op jit(solution)/shard_map/all_to_all | solution.py:189
  171.7 1.1 broadcast_in_dim.45
  172.7 10.1 %all-to-all-start.3 = ((bf16[8,258,256]{2,1,0:T(8,128)(2,1)}), bf16[8,258,256]{2,1,0:T(8,128)(2,1)}, u32[]{:S(2)}, u32[]{:S(2)}) async-start(bf16[8,258,256]{2,1,0:T(8,128)(2,1)} %broadcast_in_dim.45), calls=%async_computation.3 | async-start | bytes 2162688 | tf_op jit(solution)/shard_map/all_to_all | solution.py:185
  182.9 0.9 reduce_sum.184
  185.8 1.0 convolution_convert_fusion.2
  187.7 2.2 convolution_convert_fusion
  189.9 1.7 multiply_bitcast_fusion.2
  191.7 1.4 collective-permute-start.2
  194.7 5.3 %collective-permute-done.2 = bf16[127,256]{1,0:T(8,128)(2,1)S(1)} collective-permute-done((bf16[127,256]{1,0:T(8,128)(2,1)S(1)}, bf16[127,256]{1,0:T(8,128)(2,1)S(1)}, u32[]{:S(2)}, u32[]{:S(2)}) %collective-permute-start.2) | collective-permute-done | bytes 65056 | tf_op jit(solution)/shard_map/ppermute | solution.py:90
  200.0 0.9 maximum_maximum_fusion.dm_ref
  200.9 12.1 %shard_map.178 = (f32[256,256]{1,0:T(8,128)}, f32[128,256]{1,0:T(8,128)}) custom-call(f32[384,256]{1,0:T(8,128)} %maximum_maximum_fusion.dm_ref, f32[384,256]{1,0:T(8,128)} %maximum_convert_fusion.kv_ref, f32[128,256]{1,0:T(8,128)} %fusion.52.g_ref), custom_call_target="tpu_custom_call" | custom-call | tf_op jit(solution)/shard_map/pallas_call | solution.py:68
  213.0 1.0 multiply_bitcast_fusion.1
  214.1 1.3 collective-permute-start.3
  215.5 1.3 fusion.27
  217.4 4.4 %collective-permute-done.3 = f32[6,3,256]{2,0,1:T(8,128)S(1)} collective-permute-done((f32[6,3,256]{2,0,1:T(8,128)S(1)}, f32[6,3,256]{2,0,1:T(8,128)S(1)}, u32[]{:S(2)}, u32[]{:S(2)}) %collective-permute-start.3) | collective-permute-done | bytes 18464 | tf_op jit(solution)/shard_map/ppermute | solution.py:90
  221.9 7.1 %convolution_bitcast_fusion = f32[256,4096]{1,0:T(8,128)} fusion(bf16[3,4096,256]{2,1,0:T(8,128)(2,1)} %param.14, f32[262,3,256]{2,0,1:T(8,128)S(1)} %pad_maximum_fusion.3, f32[3,256]{1,0:T(4,128)S(1)} %copy-done.32, f32[3,256]{1,0:T(4,128)S(1)} %copy-done.34, f32[3,256]{1,0:T(4,128)S(1)} %copy-done.24, f32[3,256]{1,0:T(4,128)S(1)} %copy-done.26, ...), kind=kOutput, calls=%fused_computation.1 | convolution fusion | flops 1613758464 | bytes 16019456 | tf_op jit(solution)/shard_map/tjc,jdc->td/dot_general | solution.py:220
  229.0 5.3 %fusion.71 = (bf16[256,4096]{1,0:T(8,128)(2,1)S(1)}, f32[256]{0:T(256)S(1)}) fusion(f32[256,4096]{1,0:T(8,128)} %convolution_bitcast_fusion, f32[256,4096]{1,0:T(8,128)} %copy-done.11, f32[4096]{0:T(1024)S(1)} %get-tuple-element.113), kind=kLoop, calls=%fused_computation.179 | loop fusion | flops 4194048 | bytes 10503168 | tf_op jit(solution)/shard_map/convert_element_type | solution.py:227
  234.6 1.5 pad_maximum_fusion.2
  236.1 3.9 %all-to-all-start.4 = ((bf16[258,16,256]{2,0,1:T(8,128)(2,1)}), bf16[258,16,256]{2,0,1:T(8,128)(2,1)S(1)}, u32[]{:S(2)}, u32[]{:S(2)}) async-start(bf16[258,16,256]{2,0,1:T(8,128)(2,1)} %pad_maximum_fusion.2), calls=%async_computation.4 | async-start | bytes 4325376 | tf_op jit(solution)/shard_map/all_to_all | solution.py:232
  240.1 2.4 fusion.97
  245.4 1.1 multiply_reduce_fusion.3
  246.5 21.8 %all-to-all-done.4 = bf16[258,16,256]{2,0,1:T(8,128)(2,1)S(1)} async-done(((bf16[258,16,256]{2,0,1:T(8,128)(2,1)}), bf16[258,16,256]{2,0,1:T(8,128)(2,1)S(1)}, u32[]{:S(2)}, u32[]{:S(2)}) %all-to-all-start.4) | async-done | bytes 2113568 | tf_op jit(solution)/shard_map/all_to_all | solution.py:232
  269.1 1.7 copy-done.1
  271.7 0.9 slice_reduce_fusion.2
  273.0 1.3 broadcast_in_dim.49
  274.4 8.1 %all-to-all-start.5 = ((bf16[8,420,256]{2,1,0:T(8,128)(2,1)}), bf16[8,420,256]{2,1,0:T(8,128)(2,1)S(1)}, u32[]{:S(2)}, u32[]{:S(2)}) async-start(bf16[8,420,256]{2,1,0:T(8,128)(2,1)} %broadcast_in_dim.49), calls=%async_computation.5 | async-start | bytes 3473408 | tf_op jit(solution)/shard_map/all_to_all | solution.py:257
  282.5 2.6 slice.245
  285.0 1.1 dynamic-slice_reduce_fusion
  286.1 2.3 slice.222
  289.2 0.9 select_reduce_fusion
  290.2 31.6 %all-to-all-done.5 = bf16[8,420,256]{2,1,0:T(8,128)(2,1)S(1)} async-done(((bf16[8,420,256]{2,1,0:T(8,128)(2,1)}), bf16[8,420,256]{2,1,0:T(8,128)(2,1)S(1)}, u32[]{:S(2)}, u32[]{:S(2)}) %all-to-all-start.5) | async-done | bytes 1720352 | tf_op jit(solution)/shard_map/all_to_all | solution.py:257
  325.1 1.1 reshape.180
  327.5 1.4 fusion.14
  328.8 2.7 convolution_convert_fusion.1
  331.6 1.5 fusion.76
  333.1 6.3 %convolution_bitcast_fusion.1 = f32[3,512,256]{1,2,0:T(8,128)} fusion(bf16[3,2048,256]{2,1,0:T(8,128)(2,1)} %all-gather.8.cloned.1.call-done, f32[512]{0:T(512)S(1)} %dynamic-slice_reduce_fusion, f32[2048]{0:T(1024)S(1)} %select_reduce_fusion, s32[2048]{0:T(1024)S(1)} %bitcast.134, s32[]{:T(128)S(6)} %select_n.28, bf16[256,4096]{0,1:T(8,128)(2,1)} %copy-done.5, ...), kind=kOutput, calls=%fused_computation.24 | convolution fusion | flops 2689597440 | bytes 8931332 | tf_op jit(solution)/shard_map/td,jtc->jdc/dot_general | solution.py:284
  339.4 3.0 copy.103
  (214 shorter events, 23.1 us)
Async XLA Ops:
  7.2 60.2 %all-gather.4.cloned.1.call-start = ((), (), s32[]{:S(2)}) async-start(), calls=%async_computation.6 | async-start | bytes 3342336 | tf_op jit(solution)/shard_map/all_gather | solution.py:141
  12.5 5.8 %copy-start.38 = (f32[3,7,256]{2,1,0:T(8,128)S(1)}, f32[3,7,256]{2,1,0:T(8,128)}, u32[]{:S(2)}) copy-start(f32[3,7,256]{2,1,0:T(8,128)} %param.15) | copy-start | bytes 64516
  12.5 37.0 %all-to-all-start = ((bf16[16,256,256]{2,1,0:T(8,128)(2,1)}), bf16[16,256,256]{2,1,0:T(8,128)(2,1)}, u32[]{:S(2)}, u32[]{:S(2)}) async-start(bf16[16,256,256]{2,1,0:T(8,128)(2,1)} %broadcast_in_dim.39), calls=%async_computation | async-start | bytes 4194304 | tf_op jit(solution)/shard_map/all_to_all | solution.py:142
  18.3 139.4 %all-gather.6.cloned.1.call-start = ((), (), s32[]{:S(2)}) async-start(), calls=%async_computation.7 | async-start | bytes 2228224 | tf_op jit(solution)/shard_map/all_gather | solution.py:179
  18.4 67.0 %copy-start.23 = (f32[3,256]{1,0:T(4,128)}, f32[3,256]{1,0:T(4,128)S(1)}, u32[]{:S(2)}) copy-start(f32[3,256]{1,0:T(4,128)S(1)} %get-tuple-element.149) | copy-start | bytes 9220
  18.4 67.0 %copy-start.25 = (f32[3,256]{1,0:T(4,128)}, f32[3,256]{1,0:T(4,128)S(1)}, u32[]{:S(2)}) copy-start(f32[3,256]{1,0:T(4,128)S(1)} %get-tuple-element.150) | copy-start | bytes 9220
  18.4 67.0 %copy-start.27 = (f32[3,256]{1,0:T(4,128)}, f32[3,256]{1,0:T(4,128)S(1)}, u32[]{:S(2)}) copy-start(f32[3,256]{1,0:T(4,128)S(1)} %get-tuple-element.151) | copy-start | bytes 9220
  18.4 67.0 %copy-start.29 = (f32[3,256]{1,0:T(4,128)}, f32[3,256]{1,0:T(4,128)S(1)}, u32[]{:S(2)}) copy-start(f32[3,256]{1,0:T(4,128)S(1)} %get-tuple-element.152) | copy-start | bytes 9220
  18.4 67.0 %copy-start.31 = (f32[3,256]{1,0:T(4,128)}, f32[3,256]{1,0:T(4,128)S(1)}, u32[]{:S(2)}) copy-start(f32[3,256]{1,0:T(4,128)S(1)} %get-tuple-element.147) | copy-start | bytes 9220
  18.4 67.0 %copy-start.33 = (f32[3,256]{1,0:T(4,128)}, f32[3,256]{1,0:T(4,128)S(1)}, u32[]{:S(2)}) copy-start(f32[3,256]{1,0:T(4,128)S(1)} %get-tuple-element.148) | copy-start | bytes 9220
  52.4 17.7 %copy-start.3 = (bf16[16,256,256]{1,2,0:T(8,128)(2,1)}, bf16[16,256,256]{1,2,0:T(8,128)(2,1)S(1)}, u32[]{:S(2)}) copy-start(bf16[16,256,256]{1,2,0:T(8,128)(2,1)S(1)} %copy.94) | copy-start | bytes 6291460
  69.1 5.4 %copy-start.5 = (bf16[256,4096]{0,1:T(8,128)(2,1)}, bf16[256,4096]{0,1:T(8,128)(2,1)S(1)}, u32[]{:S(2)}) copy-start(bf16[256,4096]{0,1:T(8,128)(2,1)S(1)} %slice.226) | copy-start | bytes 6291460
  69.1 8.1 %slice-start = ((s8[6291456]{0:T(1024)(128)(4,1)}), s8[4194304]{0:T(1024)(128)(4,1)S(1)}, s32[]{:S(2)}) async-start(s8[6291456]{0:T(1024)(128)(4,1)} %bitcast.141), calls=%async_computation.9 | async-start | bytes 8388608
  70.2 4.3 %copy-start.42 = (f32[512]{0:T(512)}, f32[512]{0:T(512)S(1)}, u32[]{:S(2)}) copy-start(f32[512]{0:T(512)S(1)} %add_rsqrt_fusion) | copy-start | bytes 6148
  70.2 4.5 %copy-start = (bf16[263,4096]{0,1:T(8,128)(2,1)S(1)}, bf16[263,4096]{0,1:T(8,128)(2,1)}, u32[]{:S(2)}) copy-start(bf16[263,4096]{0,1:T(8,128)(2,1)} %all-gather.4.cloned.1.call-done) | copy-start | bytes 6463492
  70.2 7.0 %slice-start.1 = ((s8[6291456]{0:T(1024)(128)(4,1)}), s8[2097152]{0:T(1024)(128)(4,1)S(1)}, s32[]{:S(2)}) async-start(s8[6291456]{0:T(1024)(128)(4,1)} %bitcast.141), calls=%async_computation.10 | async-start | bytes 4194304
  74.5 2.7 copy-start.11
  74.7 2.5 copy-start.46
  77.2 6.8 %copy-start.57 = (f32[256]{0:T(256)S(1)}, f32[256]{0:T(256)}, u32[]{:S(2)}) copy-start(f32[256]{0:T(256)} %param.17) | copy-start | bytes 3076
  77.2 15.5 %copy-start.18 = (f32[128,256]{1,0:T(8,128)S(1)}, f32[128,256]{1,0:T(8,128)}, u32[]{:S(2)}) copy-start(f32[128,256]{1,0:T(8,128)} %param.16) | copy-start | bytes 393220
  79.1 7.9 %copy-start.13 = (bf16[256,3,256]{2,0,1:T(8,128)(2,1)}, bf16[256,3,256]{2,0,1:T(8,128)(2,1)S(1)}, u32[]{:S(2)}) copy-start(bf16[256,3,256]{2,0,1:T(8,128)(2,1)S(1)} %fusion.9) | copy-start | bytes 1179652
  79.2 6.2 %collective-permute-start = (bf16[6,3,256]{2,0,1:T(8,128)(2,1)S(1)}, bf16[6,3,256]{2,0,1:T(8,128)(2,1)S(1)}, u32[]{:S(2)}, u32[]{:S(2)}) collective-permute-start(bf16[6,3,256]{2,0,1:T(8,128)(2,1)S(1)} %slice.230), channel_id=1, source_target_pairs={{0,1},{1,2},{2,3},{3,4},{4,5},{5,6},{6,7},{8,9},{9,10},{10,11},{11... | collective-permute-start | bytes 27656 | tf_op jit(solution)/shard_map/ppermute | solution.py:90
  84.0 9.5 %copy-start.56 = (f32[128]{0:T(128)}, f32[128]{0:T(128)S(1)}, u32[]{:S(2)}) copy-start(f32[128]{0:T(128)S(1)} %iota_convert_fusion) | copy-start | bytes 1540
  84.0 17.6 %copy-start.44 = (f32[256]{0:T(256)}, f32[256]{0:T(256)S(1)}, u32[]{:S(2)}) copy-start(f32[256]{0:T(256)S(1)} %neg.7) | copy-start | bytes 3076
  84.0 3.0 copy-start.35
  87.1 7.6 %collective-permute-start.1 = (bf16[127,256]{1,0:T(8,128)(2,1)S(1)}, bf16[127,256]{1,0:T(8,128)(2,1)S(1)}, u32[]{:S(2)}, u32[]{:S(2)}) collective-permute-start(bf16[127,256]{1,0:T(8,128)(2,1)S(1)} %slice.244), channel_id=1, source_target_pairs={{0,1},{1,2},{2,3},{3,4},{4,5},{5,6},{6,7},{8,9},{9,10},{10,11},{11... | collective-permute-start | bytes 195080 | tf_op jit(solution)/shard_map/ppermute | solution.py:90
  105.7 33.0 %all-to-all-start.1 = ((bf16[256,16,256]{0,2,1:T(8,128)(2,1)}), bf16[256,16,256]{0,2,1:T(8,128)(2,1)}, u32[]{:S(2)}, u32[]{:S(2)}) async-start(bf16[256,16,256]{0,2,1:T(8,128)(2,1)} %bitcast.123), calls=%async_computation.1 | async-start | bytes 4194304 | tf_op jit(solution)/shard_map/all_to_all | solution.py:147
  112.7 48.0 %copy-start.9 = (f32[256,256]{1,0:T(8,128)}, f32[256,256]{1,0:T(8,128)S(1)}, u32[]{:S(2)}) copy-start(f32[256,256]{1,0:T(8,128)S(1)} %fusion.40) | copy-start | bytes 786436
  157.7 3.0 copy-start.40
  157.7 7.8 %copy-start.16 = (bf16[256,256]{1,0:T(8,128)(2,1)S(1)}, bf16[256,256]{1,0:T(8,128)(2,1)}, u32[]{:S(2)}) copy-start(bf16[256,256]{1,0:T(8,128)(2,1)} %multiply_convert_fusion.2) | copy-start | bytes 393220
  162.0 9.7 %all-to-all-start.2 = ((f32[16,256,4]{1,2,0:T(4,128)}), f32[16,256,4]{1,2,0:T(4,128)S(1)}, u32[]{:S(2)}, u32[]{:S(2)}) async-start(f32[16,256,4]{1,2,0:T(4,128)} %broadcast_in_dim.43), calls=%async_computation.2 | async-start | bytes 131072 | tf_op jit(solution)/shard_map/all_to_all | solution.py:189
  172.7 56.3 %all-to-all-start.3 = ((bf16[8,258,256]{2,1,0:T(8,128)(2,1)}), bf16[8,258,256]{2,1,0:T(8,128)(2,1)}, u32[]{:S(2)}, u32[]{:S(2)}) async-start(bf16[8,258,256]{2,1,0:T(8,128)(2,1)} %broadcast_in_dim.45), calls=%async_computation.3 | async-start | bytes 2162688 | tf_op jit(solution)/shard_map/all_to_all | solution.py:185
  182.9 7.0 %copy-start.12 = (f32[256,256]{1,0:T(8,128)S(1)}, f32[256,256]{1,0:T(8,128)}, u32[]{:S(2)}) copy-start(f32[256,256]{1,0:T(8,128)} %shard_map.177) | copy-start | bytes 786436
  187.7 2.2 copy-start.2
  189.9 3.2 copy-start.19
  189.9 10.1 %copy-start.50 = (f32[384]{0:T(512)S(1)}, f32[384]{0:T(512)}, u32[]{:S(2)}) copy-start(f32[384]{0:T(512)} %pad.24.clone) | copy-start | bytes 4612
  191.6 21.3 %copy-start.7 = (f32[256,3,256]{2,0,1:T(8,128)S(1)}, f32[256,3,256]{2,0,1:T(8,128)}, u32[]{:S(2)}) copy-start(f32[256,3,256]{2,0,1:T(8,128)} %copy-done.6) | copy-start | bytes 2359300
  191.7 8.3 %collective-permute-start.2 = (bf16[127,256]{1,0:T(8,128)(2,1)S(1)}, bf16[127,256]{1,0:T(8,128)(2,1)S(1)}, u32[]{:S(2)}, u32[]{:S(2)}) collective-permute-start(bf16[127,256]{1,0:T(8,128)(2,1)S(1)} %slice.398), channel_id=1, source_target_pairs={{1,0},{2,1},{3,2},{4,3},{5,4},{6,5},{7,6},{9,8},{10,9},{11,10},{12... | collective-permute-start | bytes 195080 | tf_op jit(solution)/shard_map/ppermute | solution.py:90
  200.0 15.4 %copy-start.14 = (bf16[256,3,256]{2,0,1:T(8,128)(2,1)S(1)}, bf16[256,3,256]{2,0,1:T(8,128)(2,1)}, u32[]{:S(2)}) copy-start(bf16[256,3,256]{2,0,1:T(8,128)(2,1)} %copy-done.13) | copy-start | bytes 1179652
  200.0 15.4 %copy-start.22 = (bf16[6,3,256]{2,0,1:T(8,128)(2,1)S(1)}, bf16[6,3,256]{2,0,1:T(8,128)(2,1)}, u32[]{:S(2)}) copy-start(bf16[6,3,256]{2,0,1:T(8,128)(2,1)} %copy-done.21) | copy-start | bytes 27652
  214.0 7.8 %copy-start.8 = (f32[256,1,256]{2,0,1:T(8,128)}, f32[256,1,256]{2,0,1:T(8,128)S(1)}, u32[]{:S(2)}) copy-start(f32[256,1,256]{2,0,1:T(8,128)S(1)} %get-tuple-element.122) | copy-start | bytes 786436
  214.0 7.8 %copy-start.24 = (f32[3,256]{1,0:T(4,128)S(1)}, f32[3,256]{1,0:T(4,128)}, u32[]{:S(2)}) copy-start(f32[3,256]{1,0:T(4,128)} %copy-done.23) | copy-start | bytes 9220
  214.0 7.8 %copy-start.26 = (f32[3,256]{1,0:T(4,128)S(1)}, f32[3,256]{1,0:T(4,128)}, u32[]{:S(2)}) copy-start(f32[3,256]{1,0:T(4,128)} %copy-done.25) | copy-start | bytes 9220
  214.0 7.8 %copy-start.28 = (f32[3,256]{1,0:T(4,128)S(1)}, f32[3,256]{1,0:T(4,128)}, u32[]{:S(2)}) copy-start(f32[3,256]{1,0:T(4,128)} %copy-done.27) | copy-start | bytes 9220
  214.0 7.8 %copy-start.30 = (f32[3,256]{1,0:T(4,128)S(1)}, f32[3,256]{1,0:T(4,128)}, u32[]{:S(2)}) copy-start(f32[3,256]{1,0:T(4,128)} %copy-done.29) | copy-start | bytes 9220
  214.0 7.8 %copy-start.32 = (f32[3,256]{1,0:T(4,128)S(1)}, f32[3,256]{1,0:T(4,128)}, u32[]{:S(2)}) copy-start(f32[3,256]{1,0:T(4,128)} %copy-done.31) | copy-start | bytes 9220
  214.0 7.8 %copy-start.34 = (f32[3,256]{1,0:T(4,128)S(1)}, f32[3,256]{1,0:T(4,128)}, u32[]{:S(2)}) copy-start(f32[3,256]{1,0:T(4,128)} %copy-done.33) | copy-start | bytes 9220
  214.1 7.8 %copy-start.36 = (f32[3,1,256]{2,0,1:T(4,128)S(1)}, f32[3,1,256]{2,0,1:T(4,128)}, u32[]{:S(2)}) copy-start(f32[3,1,256]{2,0,1:T(4,128)} %copy-done.35) | copy-start | bytes 9220
  214.1 7.6 %collective-permute-start.3 = (f32[6,3,256]{2,0,1:T(8,128)S(1)}, f32[6,3,256]{2,0,1:T(8,128)S(1)}, u32[]{:S(2)}, u32[]{:S(2)}) collective-permute-start(f32[6,3,256]{2,0,1:T(8,128)S(1)} %slice.247), channel_id=1, source_target_pairs={{1,0},{2,1},{3,2},{4,3},{5,4},{6,5},{7,6},{9,8},{10,9},{11,10},{12... | collective-permute-start | bytes 55304 | tf_op jit(solution)/shard_map/ppermute | solution.py:90
  236.1 3.9 %copy-start.39 = (bf16[3,7,256]{2,0,1:T(4,128)(2,1)S(1)}, bf16[3,7,256]{2,0,1:T(4,128)(2,1)}, u32[]{:S(2)}) copy-start(bf16[3,7,256]{2,0,1:T(4,128)(2,1)} %constant_dynamic-update-slice_fusion.6) | copy-start | bytes 32260
  236.1 3.9 %copy-start.52 = (bf16[3,256]{1,0:T(4,128)(2,1)S(1)}, bf16[3,256]{1,0:T(4,128)(2,1)}, u32[]{:S(2)}) copy-start(bf16[3,256]{1,0:T(4,128)(2,1)} %get-tuple-element.119) | copy-start | bytes 4612
  236.1 3.9 %copy-start.37 = (f32[3,1,256]{2,0,1:T(4,128)S(1)}, f32[3,1,256]{2,0,1:T(4,128)}, u32[]{:S(2)}) copy-start(f32[3,1,256]{2,0,1:T(4,128)} %copy-done.35) | copy-start | bytes 9220
  236.1 32.2 %all-to-all-start.4 = ((bf16[258,16,256]{2,0,1:T(8,128)(2,1)}), bf16[258,16,256]{2,0,1:T(8,128)(2,1)S(1)}, u32[]{:S(2)}, u32[]{:S(2)}) async-start(bf16[258,16,256]{2,0,1:T(8,128)(2,1)} %pad_maximum_fusion.2), calls=%async_computation.4 | async-start | bytes 4325376 | tf_op jit(solution)/shard_map/all_to_all | solution.py:232
  240.0 93.1 %all-gather.8.cloned.1.call-start = ((), (), s32[]{:S(2)}) async-start(), calls=%async_computation.8 | async-start | bytes 3538944 | tf_op jit(solution)/shard_map/all_gather | solution.py:219
  240.1 5.2 %copy-start.51 = (bf16[3,256]{1,0:T(4,128)(2,1)S(1)}, bf16[3,256]{1,0:T(4,128)(2,1)}, u32[]{:S(2)}) copy-start(bf16[3,256]{1,0:T(4,128)(2,1)} %get-tuple-element.120) | copy-start | bytes 4612
  240.1 5.3 %copy-start.45 = (f32[256]{0:T(256)S(1)}, f32[256]{0:T(256)}, u32[]{:S(2)}) copy-start(f32[256]{0:T(256)} %copy-done.44) | copy-start | bytes 3076
  268.7 2.1 copy-start.49
  268.8 2.1 copy-start.53
  268.8 2.1 copy-start.54
  268.8 3.9 %copy-start.41 = (bf16[256,4]{0,1:T(4,128)(2,1)S(1)}, bf16[256,4]{0,1:T(4,128)(2,1)}, u32[]{:S(2)}) copy-start(bf16[256,4]{0,1:T(4,128)(2,1)} %param.19) | copy-start | bytes 6148
  268.8 3.9 %copy-start.55 = (f32[256]{0:T(256)S(1)}, f32[256]{0:T(256)}, u32[]{:S(2)}) copy-start(f32[256]{0:T(256)} %param.13) | copy-start | bytes 3076
  274.4 47.4 %all-to-all-start.5 = ((bf16[8,420,256]{2,1,0:T(8,128)(2,1)}), bf16[8,420,256]{2,1,0:T(8,128)(2,1)S(1)}, u32[]{:S(2)}, u32[]{:S(2)}) async-start(bf16[8,420,256]{2,1,0:T(8,128)(2,1)} %broadcast_in_dim.49), calls=%async_computation.5 | async-start | bytes 3473408 | tf_op jit(solution)/shard_map/all_to_all | solution.py:257
  282.5 6.7 %copy-start.43 = (f32[512]{0:T(512)S(1)}, f32[512]{0:T(512)}, u32[]{:S(2)}) copy-start(f32[512]{0:T(512)} %copy-done.42) | copy-start | bytes 6148
  327.5 4.1 %copy-start.17 = (bf16[8,256,256]{2,1,0:T(8,128)(2,1)S(1)}, bf16[8,256,256]{2,1,0:T(8,128)(2,1)}, u32[]{:S(2)}) copy-start(bf16[8,256,256]{2,1,0:T(8,128)(2,1)} %slice.222) | copy-start | bytes 3145732
  (9 other events, 12.9 us)
Sparse Core Ops, SparseCore 0:
  11.1 56.1 all-gather.3
  101.8 55.8 all-gather.5
  243.1 86.9 all-gather.7
where the time goes:
time: 354 us; the launch traced here: 350 us
  waiting for transfers between devices  158 us (45%)
  starting transfers between devices  49.1 us (14%)
  local copies, waits for them, and re-layouts  44.6 us (13%)
  matrix products  34.7 us (10%)
  other arithmetic  30.2 us (9%)
  between operations  16.8 us (5%)
  Pallas kernels  16.5 us (5%)
    all_to_all x1, waiting for transfers between devices, block(): lax.all_to_all(jnp.broadcast_to(final[None], (n_ctx,) + final.shape), 'ct...  31.6 us
    all_to_all x1, waiting for transfers between devices, block(): lax.all_to_all(jnp.broadcast_to(embed[None, half:], (n_dp, vocab - half,...  31.1 us
    all_to_all x1, waiting for transfers between devices, block(): w_out_cols = lax.all_to_all(w_out_later, 'dp', 1, 0, tiled=True)  26 us
    all_to_all x1, waiting for transfers between devices, block(): du_recv = lax.all_to_all(du_send, 'dp', 1, 1, tiled=True).astype(f32)  21.8 us
    all_gather x1, waiting for transfers between devices, block(): h_full = lax.all_gather(h, 'dp', axis=1, tiled=True)  15.1 us
    all_gather x1, waiting for transfers between devices, block(): packed_full = lax.all_gather(packed, 'dp', axis=1, tiled=True)  14.9 us
    ppermute x4, starting transfers between devices, shifted(): return lax.ppermute(block, axis, route)  13.2 us
    pallas_call x1, Pallas kernels, medium_backward(): pl.pallas_call(kernel, out_shape=(jax.ShapeDtypeStruct((rows, width), jnp...  12.1 us
  transfers between devices with their start and end apart: 13, of which 11 were waited for; matrix products, arithmetic and copies ran while one was open for 19% of the time, Pallas kernels for 3%

commit v1 on v0

--- a/solution.py
+++ b/solution.py
@@ -50,19 +50,15 @@
             )
             dkv_ref[rb : rb + ROW_BLOCK, :] = acc
 
-        def lag_group(g, carry):
-            s0 = pl.multiple_of(g * 8, 8)
+        for s0 in range(0, span, 8):
             parts = []
-            for i in range(8):
-                start = span - 1 - s0 - i
+            for s in range(s0, s0 + 8):
+                start = span - 1 - s
                 part = jnp.zeros((8, LANES), jnp.float32)
                 for rb in range(0, rows, 8):
-                    part = part + dm_ref[rb : rb + 8, :] * kv_ref[pl.ds(start + rb, 8), :]
+                    part = part + dm_ref[rb : rb + 8, :] * kv_ref[start + rb : start + rb + 8, :]
                 parts.append(jnp.sum(part, axis=0, keepdims=True))
-            corr_ref[pl.ds(s0, 8), :] = jnp.concatenate(parts, axis=0)
-            return carry
-
-        lax.fori_loop(0, span // 8, lag_group, 0)
+            corr_ref[s0 : s0 + 8, :] = jnp.concatenate(parts, axis=0)
 
     ext = kv_ext.shape[0]
     return pl.pallas_call(

time: 354 us -> 349 us (0.986)
  Pallas kernels: 16.5 us -> 11.1 us
    pallas_call x1, Pallas kernels: 12.1 us -> 6.71 us  [medium_backward(): pl.pallas_call(kernel, out_shape=(jax.ShapeDtypeStruct((rows, width), jnp...]
  transfers between devices with their start and end apart: 13 -> 13, of which waited for: 11 -> 11; matrix products, arithmetic and copies ran while one was open for 19% -> 19% of each run, Pallas kernels for 3% -> 2%
where the time goes in v1:
time: 349 us; the launch traced here: 345 us
  waiting for transfers between devices  158 us (45%)
  starting transfers between devices  49.1 us (14%)
  local copies, waits for them, and re-layouts  44.6 us (13%)
  matrix products  34.7 us (10%)
  other arithmetic  30.2 us (9%)
  between operations  16.8 us (5%)
  Pallas kernels  11.1 us (3%)
    all_to_all x1, waiting for transfers between devices, block(): lax.all_to_all(jnp.broadcast_to(final[None], (n_ctx,) + final.shape), 'ct...  31.6 us
    all_to_all x1, waiting for transfers between devices, block(): lax.all_to_all(jnp.broadcast_to(embed[None, half:], (n_dp, vocab - half,...  31.1 us
    all_to_all x1, waiting for transfers between devices, block(): w_out_cols = lax.all_to_all(w_out_later, 'dp', 1, 0, tiled=True)  26 us
    all_to_all x1, waiting for transfers between devices, block(): du_recv = lax.all_to_all(du_send, 'dp', 1, 1, tiled=True).astype(f32)  21.8 us
    all_gather x1, waiting for transfers between devices, block(): h_full = lax.all_gather(h, 'dp', axis=1, tiled=True)  15.1 us
    all_gather x1, waiting for transfers between devices, block(): packed_full = lax.all_gather(packed, 'dp', axis=1, tiled=True)  14.9 us
    ppermute x4, starting transfers between devices, shifted(): return lax.ppermute(block, axis, route)  13.2 us
    ppermute x4, waiting for transfers between devices, shifted(): return lax.ppermute(block, axis, route)  12 us
  transfers between devices with their start and end apart: 13, of which 11 were waited for; matrix products, arithmetic and copies ran while one was open for 19% of the time, Pallas kernels for 2%

profile of v1, /device:TPU:0, one launch (start us, length us, event | category | flops | bytes accessed | tf_op | source)
XLA Modules:
  0.0 344.7 jit_solution(8395560734080512110)
XLA Ops:
  9.0 1.0 fusion.72
  11.0 1.5 broadcast_in_dim.39
  12.5 5.7 %all-to-all-start = ((bf16[16,256,256]{2,1,0:T(8,128)(2,1)}), bf16[16,256,256]{2,1,0:T(8,128)(2,1)}, u32[]{:S(2)}, u32[]{:S(2)}) async-start(bf16[16,256,256]{2,1,0:T(8,128)(2,1)} %broadcast_in_dim.39), calls=%async_computation | async-start | bytes 4194304 | tf_op jit(solution)/shard_map/all_to_all | solution.py:138
  18.4 31.1 %all-to-all-done = bf16[16,256,256]{2,1,0:T(8,128)(2,1)} async-done(((bf16[16,256,256]{2,1,0:T(8,128)(2,1)}), bf16[16,256,256]{2,1,0:T(8,128)(2,1)}, u32[]{:S(2)}, u32[]{:S(2)}) %all-to-all-start) | async-done | bytes 2097184 | tf_op jit(solution)/shard_map/all_to_all | solution.py:138
  49.6 2.9 copy.94
  52.4 14.9 %all-gather.4.cloned.1.call-done = bf16[263,4096]{0,1:T(8,128)(2,1)} async-done(((bf16[263,256]{0,1:T(8,128)(2,1)}), bf16[263,4096]{0,1:T(8,128)(2,1)}) %all-gather.4.cloned.1.call-update) | async-done | bytes 2154512 | tf_op jit(solution)/shard_map/all_gather | solution.py:137
  67.3 1.7 slice.226
  69.1 1.0 multiply_reduce_fusion
  70.2 4.3 %fusion.2 = f32[256,4096]{1,0:T(8,128)S(1)} fusion(bf16[256,4096]{0,1:T(8,128)(2,1)} %bitcast.121, bf16[256,4096]{0,1:T(8,128)(2,1)S(1)} %slice.226, s32[256]{0:T(256)S(1)} %copy-done.48), kind=kOutput, calls=%fused_computation.15 | convolution fusion | flops 1082261504 | bytes 8389632 | tf_op jit(solution)/shard_map/dot_general | solution.py:156
  74.7 2.5 fusion.70
  77.3 1.9 fusion.9
  79.2 4.8 %collective-permute-start = (bf16[6,3,256]{2,0,1:T(8,128)(2,1)S(1)}, bf16[6,3,256]{2,0,1:T(8,128)(2,1)S(1)}, u32[]{:S(2)}, u32[]{:S(2)}) collective-permute-start(bf16[6,3,256]{2,0,1:T(8,128)(2,1)S(1)} %slice.230), channel_id=1, source_target_pairs={{0,1},{1,2},{2,3},{3,4},{4,5},{5,6},{6,7},{8,9},{9,10},{10,11},{11... | collective-permute-start | bytes 27656 | tf_op jit(solution)/shard_map/ppermute | solution.py:86
  84.1 1.3 collective-permute-done
  86.1 0.9 copy-done.6
  87.1 5.7 %collective-permute-start.1 = (bf16[127,256]{1,0:T(8,128)(2,1)S(1)}, bf16[127,256]{1,0:T(8,128)(2,1)S(1)}, u32[]{:S(2)}, u32[]{:S(2)}) collective-permute-start(bf16[127,256]{1,0:T(8,128)(2,1)S(1)} %slice.244), channel_id=1, source_target_pairs={{0,1},{1,2},{2,3},{3,4},{4,5},{5,6},{6,7},{8,9},{9,10},{10,11},{11... | collective-permute-start | bytes 195080 | tf_op jit(solution)/shard_map/ppermute | solution.py:86
  93.6 1.0 collective-permute-done.1
  94.7 0.9 maximum_convert_fusion.kv_ref
  95.5 4.4 %shard_map.177 = f32[256,256]{1,0:T(8,128)} custom-call(f32[384,256]{1,0:T(8,128)} %maximum_convert_fusion.kv_ref, f32[128,256]{1,0:T(8,128)} %fusion.52.g_ref), custom_call_target="tpu_custom_call" | custom-call | tf_op jit(solution)/shard_map/pallas_call | solution.py:27
  99.9 1.7 multiply_convert_fusion.2
  101.7 4.1 %copy.95 = bf16[256,4096]{0,1:T(8,128)(2,1)} copy(bf16[256,4096]{1,0:T(8,128)(2,1)} %param.18) | data formatting | bytes 4194304 | tf_op jit(solution)/shard_map/optimization_barrier | solution.py:142
  105.7 4.5 %all-to-all-start.1 = ((bf16[256,16,256]{0,2,1:T(8,128)(2,1)}), bf16[256,16,256]{0,2,1:T(8,128)(2,1)}, u32[]{:S(2)}, u32[]{:S(2)}) async-start(bf16[256,16,256]{0,2,1:T(8,128)(2,1)} %bitcast.123), calls=%async_computation.1 | async-start | bytes 4194304 | tf_op jit(solution)/shard_map/all_to_all | solution.py:143
  111.5 1.2 fusion.40
  112.7 26.0 %all-to-all-done.1 = bf16[256,16,256]{0,2,1:T(8,128)(2,1)} async-done(((bf16[256,16,256]{0,2,1:T(8,128)(2,1)}), bf16[256,16,256]{0,2,1:T(8,128)(2,1)}, u32[]{:S(2)}, u32[]{:S(2)}) %all-to-all-start.1) | async-done | bytes 2097184 | tf_op jit(solution)/shard_map/all_to_all | solution.py:143
  138.7 3.9 %copy.96 = bf16[16,256,256]{2,1,0:T(8,128)(2,1)} copy(bf16[16,256,256]{1,2,0:T(8,128)(2,1)} %bitcast.8) | data formatting | bytes 4194304 | tf_op jit(solution)/shard_map/all_to_all | solution.py:143
  142.6 15.1 %all-gather.6.cloned.1.call-done = bf16[256,4096]{1,0:T(8,128)(2,1)} async-done(((bf16[256,256]{1,0:T(8,128)(2,1)}), bf16[256,4096]{1,0:T(8,128)(2,1)}) %all-gather.6.cloned.1.call-update) | async-done | bytes 2097168 | tf_op jit(solution)/shard_map/all_gather | solution.py:175
  157.7 3.0 fusion.12
  162.0 3.5 %all-to-all-start.2 = ((f32[16,256,4]{1,2,0:T(4,128)}), f32[16,256,4]{1,2,0:T(4,128)S(1)}, u32[]{:S(2)}, u32[]{:S(2)}) async-start(f32[16,256,4]{1,2,0:T(4,128)} %broadcast_in_dim.43), calls=%async_computation.2 | async-start | bytes 131072 | tf_op jit(solution)/shard_map/all_to_all | solution.py:185
  166.2 5.5 %all-to-all-done.2 = f32[16,256,4]{1,2,0:T(4,128)S(1)} async-done(((f32[16,256,4]{1,2,0:T(4,128)}), f32[16,256,4]{1,2,0:T(4,128)S(1)}, u32[]{:S(2)}, u32[]{:S(2)}) %all-to-all-start.2) | async-done | bytes 65568 | tf_op jit(solution)/shard_map/all_to_all | solution.py:185
  171.7 1.1 broadcast_in_dim.45
  172.7 10.1 %all-to-all-start.3 = ((bf16[8,258,256]{2,1,0:T(8,128)(2,1)}), bf16[8,258,256]{2,1,0:T(8,128)(2,1)}, u32[]{:S(2)}, u32[]{:S(2)}) async-start(bf16[8,258,256]{2,1,0:T(8,128)(2,1)} %broadcast_in_dim.45), calls=%async_computation.3 | async-start | bytes 2162688 | tf_op jit(solution)/shard_map/all_to_all | solution.py:181
  182.9 0.9 reduce_sum.184
  185.8 1.0 convolution_convert_fusion.2
  187.7 2.2 convolution_convert_fusion
  189.9 1.7 multiply_bitcast_fusion.2
  191.7 1.4 collective-permute-start.2
  194.7 5.3 %collective-permute-done.2 = bf16[127,256]{1,0:T(8,128)(2,1)S(1)} collective-permute-done((bf16[127,256]{1,0:T(8,128)(2,1)S(1)}, bf16[127,256]{1,0:T(8,128)(2,1)S(1)}, u32[]{:S(2)}, u32[]{:S(2)}) %collective-permute-start.2) | collective-permute-done | bytes 65056 | tf_op jit(solution)/shard_map/ppermute | solution.py:86
  200.0 0.9 maximum_maximum_fusion.dm_ref
  200.9 6.7 %shard_map.178 = (f32[256,256]{1,0:T(8,128)}, f32[128,256]{1,0:T(8,128)}) custom-call(f32[384,256]{1,0:T(8,128)} %maximum_maximum_fusion.dm_ref, f32[384,256]{1,0:T(8,128)} %maximum_convert_fusion.kv_ref, f32[128,256]{1,0:T(8,128)} %fusion.52.g_ref), custom_call_target="tpu_custom_call" | custom-call | tf_op jit(solution)/shard_map/pallas_call | solution.py:64
  207.6 1.0 multiply_bitcast_fusion.1
  208.8 1.3 collective-permute-start.3
  210.1 1.3 fusion.27
  212.0 4.4 %collective-permute-done.3 = f32[6,3,256]{2,0,1:T(8,128)S(1)} collective-permute-done((f32[6,3,256]{2,0,1:T(8,128)S(1)}, f32[6,3,256]{2,0,1:T(8,128)S(1)}, u32[]{:S(2)}, u32[]{:S(2)}) %collective-permute-start.3) | collective-permute-done | bytes 18464 | tf_op jit(solution)/shard_map/ppermute | solution.py:86
  216.5 7.1 %convolution_bitcast_fusion = f32[256,4096]{1,0:T(8,128)} fusion(bf16[3,4096,256]{2,1,0:T(8,128)(2,1)} %param.14, f32[262,3,256]{2,0,1:T(8,128)S(1)} %pad_maximum_fusion.3, f32[3,256]{1,0:T(4,128)S(1)} %copy-done.32, f32[3,256]{1,0:T(4,128)S(1)} %copy-done.34, f32[3,256]{1,0:T(4,128)S(1)} %copy-done.24, f32[3,256]{1,0:T(4,128)S(1)} %copy-done.26, ...), kind=kOutput, calls=%fused_computation.1 | convolution fusion | flops 1613758464 | bytes 16019456 | tf_op jit(solution)/shard_map/tjc,jdc->td/dot_general | solution.py:216
  223.6 5.3 %fusion.71 = (bf16[256,4096]{1,0:T(8,128)(2,1)S(1)}, f32[256]{0:T(256)S(1)}) fusion(f32[256,4096]{1,0:T(8,128)} %convolution_bitcast_fusion, f32[256,4096]{1,0:T(8,128)} %copy-done.11, f32[4096]{0:T(1024)S(1)} %get-tuple-element.113), kind=kLoop, calls=%fused_computation.179 | loop fusion | flops 4194048 | bytes 10503168 | tf_op jit(solution)/shard_map/convert_element_type | solution.py:223
  229.3 1.5 pad_maximum_fusion.2
  230.8 3.9 %all-to-all-start.4 = ((bf16[258,16,256]{2,0,1:T(8,128)(2,1)}), bf16[258,16,256]{2,0,1:T(8,128)(2,1)S(1)}, u32[]{:S(2)}, u32[]{:S(2)}) async-start(bf16[258,16,256]{2,0,1:T(8,128)(2,1)} %pad_maximum_fusion.2), calls=%async_computation.4 | async-start | bytes 4325376 | tf_op jit(solution)/shard_map/all_to_all | solution.py:228
  234.8 2.4 fusion.97
  240.0 1.1 multiply_reduce_fusion.3
  241.2 21.8 %all-to-all-done.4 = bf16[258,16,256]{2,0,1:T(8,128)(2,1)S(1)} async-done(((bf16[258,16,256]{2,0,1:T(8,128)(2,1)}), bf16[258,16,256]{2,0,1:T(8,128)(2,1)S(1)}, u32[]{:S(2)}, u32[]{:S(2)}) %all-to-all-start.4) | async-done | bytes 2113568 | tf_op jit(solution)/shard_map/all_to_all | solution.py:228
  263.7 1.7 copy-done.1
  266.3 0.9 slice_reduce_fusion.2
  267.7 1.3 broadcast_in_dim.49
  269.0 8.1 %all-to-all-start.5 = ((bf16[8,420,256]{2,1,0:T(8,128)(2,1)}), bf16[8,420,256]{2,1,0:T(8,128)(2,1)S(1)}, u32[]{:S(2)}, u32[]{:S(2)}) async-start(bf16[8,420,256]{2,1,0:T(8,128)(2,1)} %broadcast_in_dim.49), calls=%async_computation.5 | async-start | bytes 3473408 | tf_op jit(solution)/shard_map/all_to_all | solution.py:253
  277.1 2.6 slice.245
  279.7 1.1 dynamic-slice_reduce_fusion
  280.8 2.3 slice.222
  283.8 0.9 select_reduce_fusion
  284.8 31.6 %all-to-all-done.5 = bf16[8,420,256]{2,1,0:T(8,128)(2,1)S(1)} async-done(((bf16[8,420,256]{2,1,0:T(8,128)(2,1)}), bf16[8,420,256]{2,1,0:T(8,128)(2,1)S(1)}, u32[]{:S(2)}, u32[]{:S(2)}) %all-to-all-start.5) | async-done | bytes 1720352 | tf_op jit(solution)/shard_map/all_to_all | solution.py:253
  319.7 1.1 reshape.180
  322.1 1.4 fusion.14
  323.5 2.7 convolution_convert_fusion.1
  326.2 1.5 fusion.76
  327.8 6.3 %convolution_bitcast_fusion.1 = f32[3,512,256]{1,2,0:T(8,128)} fusion(bf16[3,2048,256]{2,1,0:T(8,128)(2,1)} %all-gather.8.cloned.1.call-done, f32[512]{0:T(512)S(1)} %dynamic-slice_reduce_fusion, f32[2048]{0:T(1024)S(1)} %select_reduce_fusion, s32[2048]{0:T(1024)S(1)} %bitcast.134, s32[]{:T(128)S(6)} %select_n.28, bf16[256,4096]{0,1:T(8,128)(2,1)} %copy-done.5, ...), kind=kOutput, calls=%fused_computation.24 | convolution fusion | flops 2689597440 | bytes 8931332 | tf_op jit(solution)/shard_map/td,jtc->jdc/dot_general | solution.py:280
  334.0 3.0 copy.103
  (214 shorter events, 23.1 us)
Async XLA Ops:
  7.2 60.2 %all-gather.4.cloned.1.call-start = ((), (), s32[]{:S(2)}) async-start(), calls=%async_computation.6 | async-start | bytes 3342336 | tf_op jit(solution)/shard_map/all_gather | solution.py:137
  12.5 5.8 %copy-start.38 = (f32[3,7,256]{2,1,0:T(8,128)S(1)}, f32[3,7,256]{2,1,0:T(8,128)}, u32[]{:S(2)}) copy-start(f32[3,7,256]{2,1,0:T(8,128)} %param.15) | copy-start | bytes 64516
  12.5 37.0 %all-to-all-start = ((bf16[16,256,256]{2,1,0:T(8,128)(2,1)}), bf16[16,256,256]{2,1,0:T(8,128)(2,1)}, u32[]{:S(2)}, u32[]{:S(2)}) async-start(bf16[16,256,256]{2,1,0:T(8,128)(2,1)} %broadcast_in_dim.39), calls=%async_computation | async-start | bytes 4194304 | tf_op jit(solution)/shard_map/all_to_all | solution.py:138
  18.3 139.4 %all-gather.6.cloned.1.call-start = ((), (), s32[]{:S(2)}) async-start(), calls=%async_computation.7 | async-start | bytes 2228224 | tf_op jit(solution)/shard_map/all_gather | solution.py:175
  18.4 67.0 %copy-start.23 = (f32[3,256]{1,0:T(4,128)}, f32[3,256]{1,0:T(4,128)S(1)}, u32[]{:S(2)}) copy-start(f32[3,256]{1,0:T(4,128)S(1)} %get-tuple-element.149) | copy-start | bytes 9220
  18.4 67.0 %copy-start.25 = (f32[3,256]{1,0:T(4,128)}, f32[3,256]{1,0:T(4,128)S(1)}, u32[]{:S(2)}) copy-start(f32[3,256]{1,0:T(4,128)S(1)} %get-tuple-element.150) | copy-start | bytes 9220
  18.4 67.0 %copy-start.27 = (f32[3,256]{1,0:T(4,128)}, f32[3,256]{1,0:T(4,128)S(1)}, u32[]{:S(2)}) copy-start(f32[3,256]{1,0:T(4,128)S(1)} %get-tuple-element.151) | copy-start | bytes 9220
  18.4 67.0 %copy-start.29 = (f32[3,256]{1,0:T(4,128)}, f32[3,256]{1,0:T(4,128)S(1)}, u32[]{:S(2)}) copy-start(f32[3,256]{1,0:T(4,128)S(1)} %get-tuple-element.152) | copy-start | bytes 9220
  18.4 67.0 %copy-start.31 = (f32[3,256]{1,0:T(4,128)}, f32[3,256]{1,0:T(4,128)S(1)}, u32[]{:S(2)}) copy-start(f32[3,256]{1,0:T(4,128)S(1)} %get-tuple-element.147) | copy-start | bytes 9220
  18.4 67.0 %copy-start.33 = (f32[3,256]{1,0:T(4,128)}, f32[3,256]{1,0:T(4,128)S(1)}, u32[]{:S(2)}) copy-start(f32[3,256]{1,0:T(4,128)S(1)} %get-tuple-element.148) | copy-start | bytes 9220
  52.4 17.7 %copy-start.3 = (bf16[16,256,256]{1,2,0:T(8,128)(2,1)}, bf16[16,256,256]{1,2,0:T(8,128)(2,1)S(1)}, u32[]{:S(2)}) copy-start(bf16[16,256,256]{1,2,0:T(8,128)(2,1)S(1)} %copy.94) | copy-start | bytes 6291460
  69.1 5.4 %copy-start.5 = (bf16[256,4096]{0,1:T(8,128)(2,1)}, bf16[256,4096]{0,1:T(8,128)(2,1)S(1)}, u32[]{:S(2)}) copy-start(bf16[256,4096]{0,1:T(8,128)(2,1)S(1)} %slice.226) | copy-start | bytes 6291460
  69.1 8.1 %slice-start = ((s8[6291456]{0:T(1024)(128)(4,1)}), s8[4194304]{0:T(1024)(128)(4,1)S(1)}, s32[]{:S(2)}) async-start(s8[6291456]{0:T(1024)(128)(4,1)} %bitcast.141), calls=%async_computation.9 | async-start | bytes 8388608
  70.2 4.3 %copy-start.42 = (f32[512]{0:T(512)}, f32[512]{0:T(512)S(1)}, u32[]{:S(2)}) copy-start(f32[512]{0:T(512)S(1)} %add_rsqrt_fusion) | copy-start | bytes 6148
  70.2 4.5 %copy-start = (bf16[263,4096]{0,1:T(8,128)(2,1)S(1)}, bf16[263,4096]{0,1:T(8,128)(2,1)}, u32[]{:S(2)}) copy-start(bf16[263,4096]{0,1:T(8,128)(2,1)} %all-gather.4.cloned.1.call-done) | copy-start | bytes 6463492
  70.2 7.0 %slice-start.1 = ((s8[6291456]{0:T(1024)(128)(4,1)}), s8[2097152]{0:T(1024)(128)(4,1)S(1)}, s32[]{:S(2)}) async-start(s8[6291456]{0:T(1024)(128)(4,1)} %bitcast.141), calls=%async_computation.10 | async-start | bytes 4194304
  74.5 2.7 copy-start.11
  74.7 2.5 copy-start.46
  77.2 6.8 %copy-start.57 = (f32[256]{0:T(256)S(1)}, f32[256]{0:T(256)}, u32[]{:S(2)}) copy-start(f32[256]{0:T(256)} %param.17) | copy-start | bytes 3076
  77.2 15.5 %copy-start.18 = (f32[128,256]{1,0:T(8,128)S(1)}, f32[128,256]{1,0:T(8,128)}, u32[]{:S(2)}) copy-start(f32[128,256]{1,0:T(8,128)} %param.16) | copy-start | bytes 393220
  79.1 7.9 %copy-start.13 = (bf16[256,3,256]{2,0,1:T(8,128)(2,1)}, bf16[256,3,256]{2,0,1:T(8,128)(2,1)S(1)}, u32[]{:S(2)}) copy-start(bf16[256,3,256]{2,0,1:T(8,128)(2,1)S(1)} %fusion.9) | copy-start | bytes 1179652
  79.2 6.2 %collective-permute-start = (bf16[6,3,256]{2,0,1:T(8,128)(2,1)S(1)}, bf16[6,3,256]{2,0,1:T(8,128)(2,1)S(1)}, u32[]{:S(2)}, u32[]{:S(2)}) collective-permute-start(bf16[6,3,256]{2,0,1:T(8,128)(2,1)S(1)} %slice.230), channel_id=1, source_target_pairs={{0,1},{1,2},{2,3},{3,4},{4,5},{5,6},{6,7},{8,9},{9,10},{10,11},{11... | collective-permute-start | bytes 27656 | tf_op jit(solution)/shard_map/ppermute | solution.py:86
  84.0 9.5 %copy-start.56 = (f32[128]{0:T(128)}, f32[128]{0:T(128)S(1)}, u32[]{:S(2)}) copy-start(f32[128]{0:T(128)S(1)} %iota_convert_fusion) | copy-start | bytes 1540
  84.0 17.6 %copy-start.44 = (f32[256]{0:T(256)}, f32[256]{0:T(256)S(1)}, u32[]{:S(2)}) copy-start(f32[256]{0:T(256)S(1)} %neg.7) | copy-start | bytes 3076
  84.0 3.0 copy-start.35
  87.1 7.6 %collective-permute-start.1 = (bf16[127,256]{1,0:T(8,128)(2,1)S(1)}, bf16[127,256]{1,0:T(8,128)(2,1)S(1)}, u32[]{:S(2)}, u32[]{:S(2)}) collective-permute-start(bf16[127,256]{1,0:T(8,128)(2,1)S(1)} %slice.244), channel_id=1, source_target_pairs={{0,1},{1,2},{2,3},{3,4},{4,5},{5,6},{6,7},{8,9},{9,10},{10,11},{11... | collective-permute-start | bytes 195080 | tf_op jit(solution)/shard_map/ppermute | solution.py:86
  105.7 33.0 %all-to-all-start.1 = ((bf16[256,16,256]{0,2,1:T(8,128)(2,1)}), bf16[256,16,256]{0,2,1:T(8,128)(2,1)}, u32[]{:S(2)}, u32[]{:S(2)}) async-start(bf16[256,16,256]{0,2,1:T(8,128)(2,1)} %bitcast.123), calls=%async_computation.1 | async-start | bytes 4194304 | tf_op jit(solution)/shard_map/all_to_all | solution.py:143
  112.7 48.0 %copy-start.9 = (f32[256,256]{1,0:T(8,128)}, f32[256,256]{1,0:T(8,128)S(1)}, u32[]{:S(2)}) copy-start(f32[256,256]{1,0:T(8,128)S(1)} %fusion.40) | copy-start | bytes 786436
  157.7 3.0 copy-start.40
  157.7 7.8 %copy-start.16 = (bf16[256,256]{1,0:T(8,128)(2,1)S(1)}, bf16[256,256]{1,0:T(8,128)(2,1)}, u32[]{:S(2)}) copy-start(bf16[256,256]{1,0:T(8,128)(2,1)} %multiply_convert_fusion.2) | copy-start | bytes 393220
  162.0 9.7 %all-to-all-start.2 = ((f32[16,256,4]{1,2,0:T(4,128)}), f32[16,256,4]{1,2,0:T(4,128)S(1)}, u32[]{:S(2)}, u32[]{:S(2)}) async-start(f32[16,256,4]{1,2,0:T(4,128)} %broadcast_in_dim.43), calls=%async_computation.2 | async-start | bytes 131072 | tf_op jit(solution)/shard_map/all_to_all | solution.py:185
  172.7 50.9 %all-to-all-start.3 = ((bf16[8,258,256]{2,1,0:T(8,128)(2,1)}), bf16[8,258,256]{2,1,0:T(8,128)(2,1)}, u32[]{:S(2)}, u32[]{:S(2)}) async-start(bf16[8,258,256]{2,1,0:T(8,128)(2,1)} %broadcast_in_dim.45), calls=%async_computation.3 | async-start | bytes 2162688 | tf_op jit(solution)/shard_map/all_to_all | solution.py:181
  182.9 7.0 %copy-start.12 = (f32[256,256]{1,0:T(8,128)S(1)}, f32[256,256]{1,0:T(8,128)}, u32[]{:S(2)}) copy-start(f32[256,256]{1,0:T(8,128)} %shard_map.177) | copy-start | bytes 786436
  187.7 2.2 copy-start.2
  189.9 3.2 copy-start.19
  189.9 10.1 %copy-start.50 = (f32[384]{0:T(512)S(1)}, f32[384]{0:T(512)}, u32[]{:S(2)}) copy-start(f32[384]{0:T(512)} %pad.24.clone) | copy-start | bytes 4612
  191.6 16.0 %copy-start.7 = (f32[256,3,256]{2,0,1:T(8,128)S(1)}, f32[256,3,256]{2,0,1:T(8,128)}, u32[]{:S(2)}) copy-start(f32[256,3,256]{2,0,1:T(8,128)} %copy-done.6) | copy-start | bytes 2359300
  191.7 8.3 %collective-permute-start.2 = (bf16[127,256]{1,0:T(8,128)(2,1)S(1)}, bf16[127,256]{1,0:T(8,128)(2,1)S(1)}, u32[]{:S(2)}, u32[]{:S(2)}) collective-permute-start(bf16[127,256]{1,0:T(8,128)(2,1)S(1)} %slice.398), channel_id=1, source_target_pairs={{1,0},{2,1},{3,2},{4,3},{5,4},{6,5},{7,6},{9,8},{10,9},{11,10},{12... | collective-permute-start | bytes 195080 | tf_op jit(solution)/shard_map/ppermute | solution.py:86
  200.0 10.1 %copy-start.14 = (bf16[256,3,256]{2,0,1:T(8,128)(2,1)S(1)}, bf16[256,3,256]{2,0,1:T(8,128)(2,1)}, u32[]{:S(2)}) copy-start(bf16[256,3,256]{2,0,1:T(8,128)(2,1)} %copy-done.13) | copy-start | bytes 1179652
  200.0 10.1 %copy-start.22 = (bf16[6,3,256]{2,0,1:T(8,128)(2,1)S(1)}, bf16[6,3,256]{2,0,1:T(8,128)(2,1)}, u32[]{:S(2)}) copy-start(bf16[6,3,256]{2,0,1:T(8,128)(2,1)} %copy-done.21) | copy-start | bytes 27652
  208.6 7.8 %copy-start.8 = (f32[256,1,256]{2,0,1:T(8,128)}, f32[256,1,256]{2,0,1:T(8,128)S(1)}, u32[]{:S(2)}) copy-start(f32[256,1,256]{2,0,1:T(8,128)S(1)} %get-tuple-element.122) | copy-start | bytes 786436
  208.6 7.8 %copy-start.24 = (f32[3,256]{1,0:T(4,128)S(1)}, f32[3,256]{1,0:T(4,128)}, u32[]{:S(2)}) copy-start(f32[3,256]{1,0:T(4,128)} %copy-done.23) | copy-start | bytes 9220
  208.6 7.8 %copy-start.26 = (f32[3,256]{1,0:T(4,128)S(1)}, f32[3,256]{1,0:T(4,128)}, u32[]{:S(2)}) copy-start(f32[3,256]{1,0:T(4,128)} %copy-done.25) | copy-start | bytes 9220
  208.7 7.8 %copy-start.28 = (f32[3,256]{1,0:T(4,128)S(1)}, f32[3,256]{1,0:T(4,128)}, u32[]{:S(2)}) copy-start(f32[3,256]{1,0:T(4,128)} %copy-done.27) | copy-start | bytes 9220
  208.7 7.8 %copy-start.30 = (f32[3,256]{1,0:T(4,128)S(1)}, f32[3,256]{1,0:T(4,128)}, u32[]{:S(2)}) copy-start(f32[3,256]{1,0:T(4,128)} %copy-done.29) | copy-start | bytes 9220
  208.7 7.8 %copy-start.32 = (f32[3,256]{1,0:T(4,128)S(1)}, f32[3,256]{1,0:T(4,128)}, u32[]{:S(2)}) copy-start(f32[3,256]{1,0:T(4,128)} %copy-done.31) | copy-start | bytes 9220
  208.7 7.8 %copy-start.34 = (f32[3,256]{1,0:T(4,128)S(1)}, f32[3,256]{1,0:T(4,128)}, u32[]{:S(2)}) copy-start(f32[3,256]{1,0:T(4,128)} %copy-done.33) | copy-start | bytes 9220
  208.7 7.8 %copy-start.36 = (f32[3,1,256]{2,0,1:T(4,128)S(1)}, f32[3,1,256]{2,0,1:T(4,128)}, u32[]{:S(2)}) copy-start(f32[3,1,256]{2,0,1:T(4,128)} %copy-done.35) | copy-start | bytes 9220
  208.8 7.6 %collective-permute-start.3 = (f32[6,3,256]{2,0,1:T(8,128)S(1)}, f32[6,3,256]{2,0,1:T(8,128)S(1)}, u32[]{:S(2)}, u32[]{:S(2)}) collective-permute-start(f32[6,3,256]{2,0,1:T(8,128)S(1)} %slice.247), channel_id=1, source_target_pairs={{1,0},{2,1},{3,2},{4,3},{5,4},{6,5},{7,6},{9,8},{10,9},{11,10},{12... | collective-permute-start | bytes 55304 | tf_op jit(solution)/shard_map/ppermute | solution.py:86
  230.8 3.9 %copy-start.39 = (bf16[3,7,256]{2,0,1:T(4,128)(2,1)S(1)}, bf16[3,7,256]{2,0,1:T(4,128)(2,1)}, u32[]{:S(2)}) copy-start(bf16[3,7,256]{2,0,1:T(4,128)(2,1)} %constant_dynamic-update-slice_fusion.6) | copy-start | bytes 32260
  230.8 3.9 %copy-start.52 = (bf16[3,256]{1,0:T(4,128)(2,1)S(1)}, bf16[3,256]{1,0:T(4,128)(2,1)}, u32[]{:S(2)}) copy-start(bf16[3,256]{1,0:T(4,128)(2,1)} %get-tuple-element.119) | copy-start | bytes 4612
  230.8 3.9 %copy-start.37 = (f32[3,1,256]{2,0,1:T(4,128)S(1)}, f32[3,1,256]{2,0,1:T(4,128)}, u32[]{:S(2)}) copy-start(f32[3,1,256]{2,0,1:T(4,128)} %copy-done.35) | copy-start | bytes 9220
  230.8 32.2 %all-to-all-start.4 = ((bf16[258,16,256]{2,0,1:T(8,128)(2,1)}), bf16[258,16,256]{2,0,1:T(8,128)(2,1)S(1)}, u32[]{:S(2)}, u32[]{:S(2)}) async-start(bf16[258,16,256]{2,0,1:T(8,128)(2,1)} %pad_maximum_fusion.2), calls=%async_computation.4 | async-start | bytes 4325376 | tf_op jit(solution)/shard_map/all_to_all | solution.py:228
  234.6 93.1 %all-gather.8.cloned.1.call-start = ((), (), s32[]{:S(2)}) async-start(), calls=%async_computation.8 | async-start | bytes 3538944 | tf_op jit(solution)/shard_map/all_gather | solution.py:215
  234.7 5.2 %copy-start.51 = (bf16[3,256]{1,0:T(4,128)(2,1)S(1)}, bf16[3,256]{1,0:T(4,128)(2,1)}, u32[]{:S(2)}) copy-start(bf16[3,256]{1,0:T(4,128)(2,1)} %get-tuple-element.120) | copy-start | bytes 4612
  234.7 5.3 %copy-start.45 = (f32[256]{0:T(256)S(1)}, f32[256]{0:T(256)}, u32[]{:S(2)}) copy-start(f32[256]{0:T(256)} %copy-done.44) | copy-start | bytes 3076
  263.4 2.1 copy-start.49
  263.4 2.1 copy-start.53
  263.4 2.1 copy-start.54
  263.4 3.9 %copy-start.41 = (bf16[256,4]{0,1:T(4,128)(2,1)S(1)}, bf16[256,4]{0,1:T(4,128)(2,1)}, u32[]{:S(2)}) copy-start(bf16[256,4]{0,1:T(4,128)(2,1)} %param.19) | copy-start | bytes 6148
  263.4 3.9 %copy-start.55 = (f32[256]{0:T(256)S(1)}, f32[256]{0:T(256)}, u32[]{:S(2)}) copy-start(f32[256]{0:T(256)} %param.13) | copy-start | bytes 3076
  269.0 47.4 %all-to-all-start.5 = ((bf16[8,420,256]{2,1,0:T(8,128)(2,1)}), bf16[8,420,256]{2,1,0:T(8,128)(2,1)S(1)}, u32[]{:S(2)}, u32[]{:S(2)}) async-start(bf16[8,420,256]{2,1,0:T(8,128)(2,1)} %broadcast_in_dim.49), calls=%async_computation.5 | async-start | bytes 3473408 | tf_op jit(solution)/shard_map/all_to_all | solution.py:253
  277.1 6.7 %copy-start.43 = (f32[512]{0:T(512)S(1)}, f32[512]{0:T(512)}, u32[]{:S(2)}) copy-start(f32[512]{0:T(512)} %copy-done.42) | copy-start | bytes 6148
  322.1 4.1 %copy-start.17 = (bf16[8,256,256]{2,1,0:T(8,128)(2,1)S(1)}, bf16[8,256,256]{2,1,0:T(8,128)(2,1)}, u32[]{:S(2)}) copy-start(bf16[8,256,256]{2,1,0:T(8,128)(2,1)} %slice.222) | copy-start | bytes 3145732
  (9 other events, 12.9 us)
Sparse Core Ops, SparseCore 0:
  11.1 56.1 all-gather.3
  101.8 55.8 all-gather.5
  237.8 86.9 all-gather.7

commit v2 on v1

--- a/solution.py
+++ b/solution.py
@@ -177,10 +177,6 @@
     block_out = (x0 + y).astype(bf16)
     id_hi = (ids // 32).astype(bf16)
     id_lo = (ids % 32).astype(bf16)
-    h_ids = jnp.concatenate([h, as_rows(jnp.concatenate([id_hi, id_lo]), cw)], axis=0)
-    h_ids_all = lax.all_to_all(
-        jnp.broadcast_to(h_ids[None], (n_ctx,) + h_ids.shape), "ctx", 0, 0, tiled=True
-    )
     logit_part = jnp.dot(block_out, w_tag, preferred_element_type=f32)
     logit_parts = lax.all_to_all(
         jnp.broadcast_to(logit_part[None], (n_dp,) + logit_part.shape), "dp", 0, 0, tiled=True
@@ -191,6 +187,11 @@
     tag_hot = (tags[:, None] == jnp.arange(n_tags)[None, :]).astype(f32)
     loss_part = jnp.sum(lse - jnp.sum(logits * tag_hot, axis=1))
     dlog = jnp.exp(logits - lse[:, None]) - tag_hot
+    id_dlog = jnp.concatenate([id_hi, id_lo] + split2(dlog.reshape(-1)))
+    h_ids = jnp.concatenate([h, as_rows(id_dlog, cw)], axis=0)
+    h_ids_all = lax.all_to_all(
+        jnp.broadcast_to(h_ids[None], (n_ctx,) + h_ids.shape), "ctx", 0, 0, tiled=True
+    )
     dout = jnp.dot(dlog, w_tag.astype(f32).T, precision=high)
     tag_part = jnp.dot(block_out.astype(f32).T, dlog, precision=high)
     dy_full = jnp.dot(dlog, w_tag_full_t, precision=high).astype(bf16)
@@ -244,8 +245,7 @@
         ]
     )
     n_small = small.shape[0]
-    dlog_parts = split2(dlog.reshape(-1))
-    tail = jnp.concatenate([small.astype(bf16)] + dlog_parts)
+    tail = small.astype(bf16)
     final = jnp.concatenate(
         [dx0.astype(bf16), as_rows(tail, cw)],
         axis=0,
@@ -257,13 +257,12 @@
     tail_all = final_all[:, rows:].reshape(n_ctx, -1).astype(f32)
     small_tot = jnp.sum(tail_all[:, :n_small], axis=0)
     n_dlog = rows * n_tags
-    dlog_all = (
-        tail_all[:, n_small : n_small + n_dlog] + tail_all[:, n_small + n_dlog : n_small + 2 * n_dlog]
-    ).reshape(seq, n_tags)
-
     h_all = h_ids_all[:, :rows].reshape(seq, cw)
-    id_rows = h_ids_all[:, rows:].reshape(n_ctx, -1).astype(jnp.int32)
+    extra = h_ids_all[:, rows:].reshape(n_ctx, -1)
+    id_rows = extra[:, : 2 * rows].astype(jnp.int32)
     ids_all = (id_rows[:, :rows] * 32 + id_rows[:, rows : 2 * rows]).reshape(seq)
+    dlog_rows = extra[:, 2 * rows : 2 * rows + 2 * n_dlog].astype(f32)
+    dlog_all = (dlog_rows[:, :n_dlog] + dlog_rows[:, n_dlog:]).reshape(seq, n_tags)
 
     f_cols = width // n_ctx
     w_tag_cols = lax.dynamic_slice_in_dim(w_tag_full_t, k_ctx * f_cols, f_cols, 1)

time: 349 us -> 331 us (0.948)
  waiting for transfers between devices: 158 us -> 143 us
    all_to_all x1, waiting for transfers between devices: 31.6 us -> 18.4 us  [block(): lax.all_to_all(jnp.broadcast_to(final[None], (n_ctx,) + final.shape), 'ct...]
    all_to_all x1, waiting for transfers between devices: 21.8 us -> 27.4 us  [block(): du_recv = lax.all_to_all(du_send, 'dp', 1, 1, tiled=True).astype(f32)]
    ppermute x4, waiting for transfers between devices: 12 us -> 7.79 us  [shifted(): return lax.ppermute(block, axis, route)]
    unnamed x138 -> x136, local copies, waits for them, and re-layouts: 11.5 us -> 10.5 us
  transfers between devices with their start and end apart: 13 -> 13, of which waited for: 11 -> 10; matrix products, arithmetic and copies ran while one was open for 19% -> 19% of each run, Pallas kernels for 2% -> 2%
where the time goes in v2:
time: 331 us; the launch traced here: 329 us
  waiting for transfers between devices  143 us (43%)
  starting transfers between devices  52 us (16%)
  local copies, waits for them, and re-layouts  42.8 us (13%)
  matrix products  34.1 us (10%)
  other arithmetic  29.1 us (9%)
  between operations  16.8 us (5%)
  Pallas kernels  11.1 us (3%)
    all_to_all x1, waiting for transfers between devices, block(): lax.all_to_all(jnp.broadcast_to(embed[None, half:], (n_dp, vocab - half,...  31.2 us
    all_to_all x1, waiting for transfers between devices, block(): du_recv = lax.all_to_all(du_send, 'dp', 1, 1, tiled=True).astype(f32)  27.4 us
    all_to_all x1, waiting for transfers between devices, block(): w_out_cols = lax.all_to_all(w_out_later, 'dp', 1, 0, tiled=True)  26 us
    all_to_all x1, waiting for transfers between devices, block(): lax.all_to_all(jnp.broadcast_to(final[None], (n_ctx,) + final.shape), 'ct...  18.4 us
    all_gather x1, waiting for transfers between devices, block(): h_full = lax.all_gather(h, 'dp', axis=1, tiled=True)  15.1 us
    all_gather x1, waiting for transfers between devices, block(): packed_full = lax.all_gather(packed, 'dp', axis=1, tiled=True)  14.9 us
    ppermute x4, starting transfers between devices, shifted(): return lax.ppermute(block, axis, route)  13.1 us
    all_to_all x1, starting transfers between devices, block(): lax.all_to_all(jnp.broadcast_to(h_ids[None], (n_ctx,) + h_ids.shape), 'ct...  11.6 us
  transfers between devices with their start and end apart: 13, of which 10 were waited for; matrix products, arithmetic and copies ran while one was open for 19% of the time, Pallas kernels for 2%

profile of v2, /device:TPU:0, one launch (start us, length us, event | category | flops | bytes accessed | tf_op | source)
XLA Modules:
  0.0 329.1 jit_solution(5299144192100135674)
XLA Ops:
  8.2 0.8 copy.95
  9.0 1.0 fusion.72
  10.1 0.8 concatenate.38
  11.0 1.5 broadcast_in_dim.39
  12.5 5.7 %all-to-all-start = ((bf16[16,256,256]{2,1,0:T(8,128)(2,1)}), bf16[16,256,256]{2,1,0:T(8,128)(2,1)}, u32[]{:S(2)}, u32[]{:S(2)}) async-start(bf16[16,256,256]{2,1,0:T(8,128)(2,1)} %broadcast_in_dim.39), calls=%async_computation | async-start | bytes 4194304 | tf_op jit(solution)/shard_map/all_to_all | solution.py:138
  18.4 31.2 %all-to-all-done = bf16[16,256,256]{2,1,0:T(8,128)(2,1)} async-done(((bf16[16,256,256]{2,1,0:T(8,128)(2,1)}), bf16[16,256,256]{2,1,0:T(8,128)(2,1)}, u32[]{:S(2)}, u32[]{:S(2)}) %all-to-all-start) | async-done | bytes 2097184 | tf_op jit(solution)/shard_map/all_to_all | solution.py:138
  49.6 2.9 copy.99
  52.5 14.9 %all-gather.4.cloned.1.call-done = bf16[263,4096]{0,1:T(8,128)(2,1)} async-done(((bf16[263,256]{0,1:T(8,128)(2,1)}), bf16[263,4096]{0,1:T(8,128)(2,1)}) %all-gather.4.cloned.1.call-update) | async-done | bytes 2154512 | tf_op jit(solution)/shard_map/all_gather | solution.py:137
  67.3 1.7 slice.238
  69.1 1.0 multiply_reduce_fusion
  70.2 4.3 %fusion.2 = f32[256,4096]{1,0:T(8,128)S(1)} fusion(bf16[256,4096]{0,1:T(8,128)(2,1)} %bitcast.119, bf16[256,4096]{0,1:T(8,128)(2,1)S(1)} %slice.238, s32[256]{0:T(256)S(1)} %copy-done.44), kind=kOutput, calls=%fused_computation.15 | convolution fusion | flops 1082261504 | bytes 8389632 | tf_op jit(solution)/shard_map/dot_general | solution.py:156
  74.7 2.5 fusion.70
  77.3 1.9 fusion.9
  79.2 4.8 %collective-permute-start = (bf16[6,3,256]{2,0,1:T(8,128)(2,1)S(1)}, bf16[6,3,256]{2,0,1:T(8,128)(2,1)S(1)}, u32[]{:S(2)}, u32[]{:S(2)}) collective-permute-start(bf16[6,3,256]{2,0,1:T(8,128)(2,1)S(1)} %slice.242), channel_id=1, source_target_pairs={{0,1},{1,2},{2,3},{3,4},{4,5},{5,6},{6,7},{8,9},{9,10},{10,11},{11... | collective-permute-start | bytes 27656 | tf_op jit(solution)/shard_map/ppermute | solution.py:86
  84.1 1.3 collective-permute-done
  86.1 0.9 copy-done.7
  87.1 5.7 %collective-permute-start.1 = (bf16[127,256]{1,0:T(8,128)(2,1)S(1)}, bf16[127,256]{1,0:T(8,128)(2,1)S(1)}, u32[]{:S(2)}, u32[]{:S(2)}) collective-permute-start(bf16[127,256]{1,0:T(8,128)(2,1)S(1)} %slice.256), channel_id=1, source_target_pairs={{0,1},{1,2},{2,3},{3,4},{4,5},{5,6},{6,7},{8,9},{9,10},{10,11},{11... | collective-permute-start | bytes 195080 | tf_op jit(solution)/shard_map/ppermute | solution.py:86
  93.6 1.0 collective-permute-done.1
  94.6 0.9 maximum_convert_fusion.kv_ref
  95.5 4.4 %shard_map.177 = f32[256,256]{1,0:T(8,128)} custom-call(f32[384,256]{1,0:T(8,128)} %maximum_convert_fusion.kv_ref, f32[128,256]{1,0:T(8,128)} %fusion.52.g_ref), custom_call_target="tpu_custom_call" | custom-call | tf_op jit(solution)/shard_map/pallas_call | solution.py:27
  99.9 1.7 multiply_convert_fusion.2
  101.7 4.1 %copy.100 = bf16[256,4096]{0,1:T(8,128)(2,1)} copy(bf16[256,4096]{1,0:T(8,128)(2,1)} %param.18) | data formatting | bytes 4194304 | tf_op jit(solution)/shard_map/optimization_barrier | solution.py:142
  105.8 4.4 %all-to-all-start.1 = ((bf16[256,16,256]{0,2,1:T(8,128)(2,1)}), bf16[256,16,256]{0,2,1:T(8,128)(2,1)}, u32[]{:S(2)}, u32[]{:S(2)}) async-start(bf16[256,16,256]{0,2,1:T(8,128)(2,1)} %bitcast.121), calls=%async_computation.1 | async-start | bytes 4194304 | tf_op jit(solution)/shard_map/all_to_all | solution.py:143
  111.5 1.2 fusion.40
  112.7 26.0 %all-to-all-done.1 = bf16[256,16,256]{0,2,1:T(8,128)(2,1)} async-done(((bf16[256,16,256]{0,2,1:T(8,128)(2,1)}), bf16[256,16,256]{0,2,1:T(8,128)(2,1)}, u32[]{:S(2)}, u32[]{:S(2)}) %all-to-all-start.1) | async-done | bytes 2097184 | tf_op jit(solution)/shard_map/all_to_all | solution.py:143
  138.7 3.9 %copy.101 = bf16[16,256,256]{2,1,0:T(8,128)(2,1)} copy(bf16[16,256,256]{1,2,0:T(8,128)(2,1)} %bitcast.8) | data formatting | bytes 4194304 | tf_op jit(solution)/shard_map/all_to_all | solution.py:143
  142.7 15.1 %all-gather.6.cloned.1.call-done = bf16[256,4096]{1,0:T(8,128)(2,1)} async-done(((bf16[256,256]{1,0:T(8,128)(2,1)}), bf16[256,4096]{1,0:T(8,128)(2,1)}) %all-gather.6.cloned.1.call-update) | async-done | bytes 2097168 | tf_op jit(solution)/shard_map/all_gather | solution.py:175
  157.7 2.9 fusion.12
  161.5 4.3 %all-to-all-start.2 = ((f32[16,256,4]{1,2,0:T(4,128)}), f32[16,256,4]{1,2,0:T(4,128)}, u32[]{:S(2)}, u32[]{:S(2)}) async-start(f32[16,256,4]{1,2,0:T(4,128)} %broadcast_in_dim.43), calls=%async_computation.2 | async-start | bytes 131072 | tf_op jit(solution)/shard_map/all_to_all | solution.py:181
  166.4 1.3 slice.257
  167.7 1.7 dynamic-slice_reduce_fusion
  169.4 2.4 all-to-all-done.2
  171.8 0.9 reduce_sum.184
  174.9 0.8 copy.102
  175.7 2.2 convolution_convert_fusion
  178.0 1.7 multiply_bitcast_fusion.2
  180.6 1.3 collective-permute-start.2
  182.1 1.1 broadcast_in_dim.45
  183.2 11.6 %all-to-all-start.3 = ((bf16[8,266,256]{2,1,0:T(8,128)(2,1)}), bf16[8,266,256]{2,1,0:T(8,128)(2,1)S(1)}, u32[]{:S(2)}, u32[]{:S(2)}) async-start(bf16[8,266,256]{2,1,0:T(8,128)(2,1)} %broadcast_in_dim.45), calls=%async_computation.3 | async-start | bytes 2228224 | tf_op jit(solution)/shard_map/all_to_all | solution.py:192
  194.9 0.9 maximum_maximum_fusion.dm_ref
  195.8 6.7 %shard_map.178 = (f32[256,256]{1,0:T(8,128)}, f32[128,256]{1,0:T(8,128)}) custom-call(f32[384,256]{1,0:T(8,128)} %maximum_maximum_fusion.dm_ref, f32[384,256]{1,0:T(8,128)} %maximum_convert_fusion.kv_ref, f32[128,256]{1,0:T(8,128)} %fusion.52.g_ref), custom_call_target="tpu_custom_call" | custom-call | tf_op jit(solution)/shard_map/pallas_call | solution.py:64
  202.5 1.0 multiply_bitcast_fusion.1
  203.6 1.3 collective-permute-start.3
  205.7 5.4 %collective-permute-done.3 = f32[6,3,256]{2,0,1:T(8,128)S(1)} collective-permute-done((f32[6,3,256]{2,0,1:T(8,128)S(1)}, f32[6,3,256]{2,0,1:T(8,128)S(1)}, u32[]{:S(2)}, u32[]{:S(2)}) %collective-permute-start.3) | collective-permute-done | bytes 18464 | tf_op jit(solution)/shard_map/ppermute | solution.py:86
  211.2 1.4 fusion.97
  212.7 7.1 %convolution_bitcast_fusion = f32[256,4096]{1,0:T(8,128)} fusion(bf16[3,4096,256]{2,1,0:T(8,128)(2,1)} %param.14, f32[262,3,256]{2,0,1:T(8,128)S(1)} %pad_maximum_fusion.3, f32[3,256]{1,0:T(4,128)S(1)} %copy-done.30, f32[3,256]{1,0:T(4,128)S(1)} %copy-done.32, f32[3,256]{1,0:T(4,128)S(1)} %get-tuple-element.149, f32[3,256]{1,0:T(4,128)S(1)} %get-tuple-element.150, ...), kind=kOutput, calls=%fused_computation.1 | convolution fusion | flops 1613758464 | bytes 16019456 | tf_op jit(solution)/shard_map/tjc,jdc->td/dot_general | solution.py:217
  219.8 6.1 %fusion.71 = (bf16[256,4096]{1,0:T(8,128)(2,1)S(1)}, f32[256]{0:T(256)S(1)}) fusion(f32[256,4096]{1,0:T(8,128)} %convolution_bitcast_fusion, f32[256,4096]{1,0:T(8,128)} %copy-done.10, f32[4096]{0:T(1024)S(1)} %copy-done.22), kind=kLoop, calls=%fused_computation.180 | loop fusion | flops 4194048 | bytes 10503168 | tf_op jit(solution)/shard_map/convert_element_type | solution.py:224
  226.2 1.5 pad_maximum_fusion.2
  227.7 4.8 %all-to-all-start.4 = ((bf16[258,16,256]{2,0,1:T(8,128)(2,1)}), bf16[258,16,256]{2,0,1:T(8,128)(2,1)}, u32[]{:S(2)}, u32[]{:S(2)}) async-start(bf16[258,16,256]{2,0,1:T(8,128)(2,1)} %pad_maximum_fusion.2), calls=%async_computation.4 | async-start | bytes 4325376 | tf_op jit(solution)/shard_map/all_to_all | solution.py:229
  233.3 27.4 %all-to-all-done.4 = bf16[258,16,256]{2,0,1:T(8,128)(2,1)} async-done(((bf16[258,16,256]{2,0,1:T(8,128)(2,1)}), bf16[258,16,256]{2,0,1:T(8,128)(2,1)}, u32[]{:S(2)}, u32[]{:S(2)}) %all-to-all-start.4) | async-done | bytes 2113568 | tf_op jit(solution)/shard_map/all_to_all | solution.py:229
  260.7 1.9 convert_element_type.196
  263.0 1.7 copy-done.1
  267.5 0.9 slice_reduce_fusion.1
  268.8 1.3 broadcast_in_dim.49
  270.1 7.9 %all-to-all-start.5 = ((bf16[8,412,256]{2,1,0:T(8,128)(2,1)}), bf16[8,412,256]{2,1,0:T(8,128)(2,1)S(1)}, u32[]{:S(2)}, u32[]{:S(2)}) async-start(bf16[8,412,256]{2,1,0:T(8,128)(2,1)} %broadcast_in_dim.49), calls=%async_computation.5 | async-start | bytes 3407872 | tf_op jit(solution)/shard_map/all_to_all | solution.py:253
  278.1 2.1 reshape.181
  280.1 0.9 select_reduce_fusion
  281.0 3.0 convolution_convert_fusion.1
  284.1 1.5 fusion.76
  285.6 18.4 %all-to-all-done.5 = bf16[8,412,256]{2,1,0:T(8,128)(2,1)S(1)} async-done(((bf16[8,412,256]{2,1,0:T(8,128)(2,1)}), bf16[8,412,256]{2,1,0:T(8,128)(2,1)S(1)}, u32[]{:S(2)}, u32[]{:S(2)}) %all-to-all-start.5) | async-done | bytes 1687584 | tf_op jit(solution)/shard_map/all_to_all | solution.py:253
  309.0 1.3 slice.277
  310.9 1.4 fusion.14
  312.3 6.2 %convolution_bitcast_fusion.1 = f32[3,512,256]{1,2,0:T(8,128)} fusion(bf16[3,2048,256]{2,1,0:T(8,128)(2,1)} %all-gather.8.cloned.1.call-done, f32[512]{0:T(512)S(1)} %copy-done.48, f32[2048]{0:T(1024)S(1)} %select_reduce_fusion, s32[2048]{0:T(1024)S(1)} %bitcast.133, s32[]{:T(128)S(6)} %select_n.28, bf16[256,4096]{0,1:T(8,128)(2,1)} %copy-done.6, ...), kind=kOutput, calls=%fused_computation.24 | convolution fusion | flops 2689597440 | bytes 8931332 | tf_op jit(solution)/shard_map/td,jtc->jdc/dot_general | solution.py:279
  318.5 3.0 copy.109
  (216 shorter events, 19.1 us)
Async XLA Ops:
  7.2 60.1 %all-gather.4.cloned.1.call-start = ((), (), s32[]{:S(2)}) async-start(), calls=%async_computation.6 | async-start | bytes 3342336 | tf_op jit(solution)/shard_map/all_gather | solution.py:137
  12.5 5.8 %copy-start.35 = (f32[3,7,256]{2,1,0:T(8,128)S(1)}, f32[3,7,256]{2,1,0:T(8,128)}, u32[]{:S(2)}) copy-start(f32[3,7,256]{2,1,0:T(8,128)} %param.15) | copy-start | bytes 64516
  12.5 37.1 %all-to-all-start = ((bf16[16,256,256]{2,1,0:T(8,128)(2,1)}), bf16[16,256,256]{2,1,0:T(8,128)(2,1)}, u32[]{:S(2)}, u32[]{:S(2)}) async-start(bf16[16,256,256]{2,1,0:T(8,128)(2,1)} %broadcast_in_dim.39), calls=%async_computation | async-start | bytes 4194304 | tf_op jit(solution)/shard_map/all_to_all | solution.py:138
  18.2 139.5 %all-gather.6.cloned.1.call-start = ((), (), s32[]{:S(2)}) async-start(), calls=%async_computation.7 | async-start | bytes 2228224 | tf_op jit(solution)/shard_map/all_gather | solution.py:175
  18.3 67.0 %copy-start.25 = (f32[3,256]{1,0:T(4,128)}, f32[3,256]{1,0:T(4,128)S(1)}, u32[]{:S(2)}) copy-start(f32[3,256]{1,0:T(4,128)S(1)} %get-tuple-element.151) | copy-start | bytes 9220
  18.4 67.0 %copy-start.27 = (f32[3,256]{1,0:T(4,128)}, f32[3,256]{1,0:T(4,128)S(1)}, u32[]{:S(2)}) copy-start(f32[3,256]{1,0:T(4,128)S(1)} %get-tuple-element.152) | copy-start | bytes 9220
  18.4 67.0 %copy-start.29 = (f32[3,256]{1,0:T(4,128)}, f32[3,256]{1,0:T(4,128)S(1)}, u32[]{:S(2)}) copy-start(f32[3,256]{1,0:T(4,128)S(1)} %get-tuple-element.147) | copy-start | bytes 9220
  18.4 67.0 %copy-start.31 = (f32[3,256]{1,0:T(4,128)}, f32[3,256]{1,0:T(4,128)S(1)}, u32[]{:S(2)}) copy-start(f32[3,256]{1,0:T(4,128)S(1)} %get-tuple-element.148) | copy-start | bytes 9220
  52.4 17.7 %copy-start.4 = (bf16[16,256,256]{1,2,0:T(8,128)(2,1)}, bf16[16,256,256]{1,2,0:T(8,128)(2,1)S(1)}, u32[]{:S(2)}) copy-start(bf16[16,256,256]{1,2,0:T(8,128)(2,1)S(1)} %copy.99) | copy-start | bytes 6291460
  69.1 5.4 %copy-start.6 = (bf16[256,4096]{0,1:T(8,128)(2,1)}, bf16[256,4096]{0,1:T(8,128)(2,1)S(1)}, u32[]{:S(2)}) copy-start(bf16[256,4096]{0,1:T(8,128)(2,1)S(1)} %slice.238) | copy-start | bytes 6291460
  69.1 8.2 %slice-start.1 = ((s8[6291456]{0:T(1024)(128)(4,1)}), s8[4194304]{0:T(1024)(128)(4,1)S(1)}, s32[]{:S(2)}) async-start(s8[6291456]{0:T(1024)(128)(4,1)} %bitcast.139), calls=%async_computation.10 | async-start | bytes 8388608
  70.1 4.3 %copy-start.38 = (f32[512]{0:T(512)}, f32[512]{0:T(512)S(1)}, u32[]{:S(2)}) copy-start(f32[512]{0:T(512)S(1)} %add_rsqrt_fusion) | copy-start | bytes 6148
  70.2 4.5 %copy-start = (bf16[263,4096]{0,1:T(8,128)(2,1)S(1)}, bf16[263,4096]{0,1:T(8,128)(2,1)}, u32[]{:S(2)}) copy-start(bf16[263,4096]{0,1:T(8,128)(2,1)} %all-gather.4.cloned.1.call-done) | copy-start | bytes 6463492
  70.2 7.1 %slice-start.2 = ((s8[6291456]{0:T(1024)(128)(4,1)}), s8[2097152]{0:T(1024)(128)(4,1)S(1)}, s32[]{:S(2)}) async-start(s8[6291456]{0:T(1024)(128)(4,1)} %bitcast.139), calls=%async_computation.11 | async-start | bytes 4194304
  74.5 2.8 copy-start.10
  74.7 2.6 copy-start.42
  77.3 6.7 %copy-start.53 = (f32[256]{0:T(256)S(1)}, f32[256]{0:T(256)}, u32[]{:S(2)}) copy-start(f32[256]{0:T(256)} %param.17) | copy-start | bytes 3076
  77.3 15.5 %copy-start.16 = (f32[128,256]{1,0:T(8,128)S(1)}, f32[128,256]{1,0:T(8,128)}, u32[]{:S(2)}) copy-start(f32[128,256]{1,0:T(8,128)} %param.16) | copy-start | bytes 393220
  79.2 7.8 %copy-start.12 = (bf16[256,3,256]{2,0,1:T(8,128)(2,1)}, bf16[256,3,256]{2,0,1:T(8,128)(2,1)S(1)}, u32[]{:S(2)}) copy-start(bf16[256,3,256]{2,0,1:T(8,128)(2,1)S(1)} %fusion.9) | copy-start | bytes 1179652
  79.2 6.2 %collective-permute-start = (bf16[6,3,256]{2,0,1:T(8,128)(2,1)S(1)}, bf16[6,3,256]{2,0,1:T(8,128)(2,1)S(1)}, u32[]{:S(2)}, u32[]{:S(2)}) collective-permute-start(bf16[6,3,256]{2,0,1:T(8,128)(2,1)S(1)} %slice.242), channel_id=1, source_target_pairs={{0,1},{1,2},{2,3},{3,4},{4,5},{5,6},{6,7},{8,9},{9,10},{10,11},{11... | collective-permute-start | bytes 27656 | tf_op jit(solution)/shard_map/ppermute | solution.py:86
  84.0 17.6 %copy-start.49 = (f32[128]{0:T(128)}, f32[128]{0:T(128)S(1)}, u32[]{:S(2)}) copy-start(f32[128]{0:T(128)S(1)} %iota_convert_fusion) | copy-start | bytes 1540
  84.0 17.6 %copy-start.40 = (f32[256]{0:T(256)}, f32[256]{0:T(256)S(1)}, u32[]{:S(2)}) copy-start(f32[256]{0:T(256)S(1)} %neg.7) | copy-start | bytes 3076
  84.1 17.6 %copy-start.33 = (f32[3,1,256]{2,0,1:T(4,128)}, f32[3,1,256]{2,0,1:T(4,128)S(1)}, u32[]{:S(2)}) copy-start(f32[3,1,256]{2,0,1:T(4,128)S(1)} %copy.133) | copy-start | bytes 9220
  85.4 9.3 %copy-start.23 = (bf16[6,3,256]{2,0,1:T(8,128)(2,1)}, bf16[6,3,256]{2,0,1:T(8,128)(2,1)S(1)}, u32[]{:S(2)}) copy-start(bf16[6,3,256]{2,0,1:T(8,128)(2,1)S(1)} %collective-permute-done) | copy-start | bytes 27652
  87.1 7.6 %collective-permute-start.1 = (bf16[127,256]{1,0:T(8,128)(2,1)S(1)}, bf16[127,256]{1,0:T(8,128)(2,1)S(1)}, u32[]{:S(2)}, u32[]{:S(2)}) collective-permute-start(bf16[127,256]{1,0:T(8,128)(2,1)S(1)} %slice.256), channel_id=1, source_target_pairs={{0,1},{1,2},{2,3},{3,4},{4,5},{5,6},{6,7},{8,9},{9,10},{10,11},{11... | collective-permute-start | bytes 195080 | tf_op jit(solution)/shard_map/ppermute | solution.py:86
  105.8 33.0 %all-to-all-start.1 = ((bf16[256,16,256]{0,2,1:T(8,128)(2,1)}), bf16[256,16,256]{0,2,1:T(8,128)(2,1)}, u32[]{:S(2)}, u32[]{:S(2)}) async-start(bf16[256,16,256]{0,2,1:T(8,128)(2,1)} %bitcast.121), calls=%async_computation.1 | async-start | bytes 4194304 | tf_op jit(solution)/shard_map/all_to_all | solution.py:143
  157.7 3.0 copy-start.36
  160.7 17.2 %copy-start.14 = (bf16[256,256]{1,0:T(8,128)(2,1)}, bf16[256,256]{1,0:T(8,128)(2,1)S(1)}, u32[]{:S(2)}) copy-start(bf16[256,256]{1,0:T(8,128)(2,1)S(1)} %fusion.12) | copy-start | bytes 393220
  161.5 10.3 %all-to-all-start.2 = ((f32[16,256,4]{1,2,0:T(4,128)}), f32[16,256,4]{1,2,0:T(4,128)}, u32[]{:S(2)}, u32[]{:S(2)}) async-start(f32[16,256,4]{1,2,0:T(4,128)} %broadcast_in_dim.43), calls=%async_computation.2 | async-start | bytes 131072 | tf_op jit(solution)/shard_map/all_to_all | solution.py:181
  175.7 2.2 copy-start.3
  175.7 2.2 copy-start.11
  177.9 4.0 %copy-start.18 = (f32[256,4]{1,0:T(8,128)S(1)}, f32[256,4]{1,0:T(8,128)}, u32[]{:S(2)}) copy-start(f32[256,4]{1,0:T(8,128)} %copy.102) | copy-start | bytes 12292
  177.9 4.1 %copy-start.51 = (bf16[256]{0:T(256)(128)(2,1)S(1)}, bf16[256]{0:T(256)(128)(2,1)}, u32[]{:S(2)}) copy-start(bf16[256]{0:T(256)(128)(2,1)} %get-tuple-element.142) | copy-start | bytes 1540
  177.9 4.1 %copy-start.52 = (bf16[256]{0:T(256)(128)(2,1)S(1)}, bf16[256]{0:T(256)(128)(2,1)}, u32[]{:S(2)}) copy-start(bf16[256]{0:T(256)(128)(2,1)} %get-tuple-element.143) | copy-start | bytes 1540
  177.9 4.1 %copy-start.15 = (bf16[256,256]{1,0:T(8,128)(2,1)S(1)}, bf16[256,256]{1,0:T(8,128)(2,1)}, u32[]{:S(2)}) copy-start(bf16[256,256]{1,0:T(8,128)(2,1)} %multiply_convert_fusion.2) | copy-start | bytes 393220
  179.9 15.0 %copy-start.45 = (f32[384]{0:T(512)S(1)}, f32[384]{0:T(512)}, u32[]{:S(2)}) copy-start(f32[384]{0:T(512)} %pad.26.clone) | copy-start | bytes 4612
  180.6 14.2 %collective-permute-start.2 = (bf16[127,256]{1,0:T(8,128)(2,1)S(1)}, bf16[127,256]{1,0:T(8,128)(2,1)S(1)}, u32[]{:S(2)}, u32[]{:S(2)}) collective-permute-start(bf16[127,256]{1,0:T(8,128)(2,1)S(1)} %slice.415), channel_id=1, source_target_pairs={{1,0},{2,1},{3,2},{4,3},{5,4},{6,5},{7,6},{9,8},{10,9},{11,10},{12... | collective-permute-start | bytes 195080 | tf_op jit(solution)/shard_map/ppermute | solution.py:86
  183.2 19.3 %copy-start.8 = (f32[256,3,256]{2,0,1:T(8,128)S(1)}, f32[256,3,256]{2,0,1:T(8,128)}, u32[]{:S(2)}) copy-start(f32[256,3,256]{2,0,1:T(8,128)} %copy-done.7) | copy-start | bytes 2359300
  183.2 36.6 %all-to-all-start.3 = ((bf16[8,266,256]{2,1,0:T(8,128)(2,1)}), bf16[8,266,256]{2,1,0:T(8,128)(2,1)S(1)}, u32[]{:S(2)}, u32[]{:S(2)}) async-start(bf16[8,266,256]{2,1,0:T(8,128)(2,1)} %broadcast_in_dim.45), calls=%async_computation.3 | async-start | bytes 2228224 | tf_op jit(solution)/shard_map/all_to_all | solution.py:192
  194.8 117.5 %all-gather.8.cloned.1.call-start = ((), (), s32[]{:S(2)}) async-start(), calls=%async_computation.8 | async-start | bytes 3538944 | tf_op jit(solution)/shard_map/all_gather | solution.py:216
  194.9 10.0 %copy-start.13 = (bf16[256,3,256]{2,0,1:T(8,128)(2,1)S(1)}, bf16[256,3,256]{2,0,1:T(8,128)(2,1)}, u32[]{:S(2)}) copy-start(bf16[256,3,256]{2,0,1:T(8,128)(2,1)} %copy-done.12) | copy-start | bytes 1179652
  194.9 10.0 %copy-start.24 = (bf16[6,3,256]{2,0,1:T(8,128)(2,1)S(1)}, bf16[6,3,256]{2,0,1:T(8,128)(2,1)}, u32[]{:S(2)}) copy-start(bf16[6,3,256]{2,0,1:T(8,128)(2,1)} %copy-done.23) | copy-start | bytes 27652
  203.5 7.7 %copy-start.26 = (f32[3,256]{1,0:T(4,128)S(1)}, f32[3,256]{1,0:T(4,128)}, u32[]{:S(2)}) copy-start(f32[3,256]{1,0:T(4,128)} %copy-done.25) | copy-start | bytes 9220
  203.5 7.7 %copy-start.28 = (f32[3,256]{1,0:T(4,128)S(1)}, f32[3,256]{1,0:T(4,128)}, u32[]{:S(2)}) copy-start(f32[3,256]{1,0:T(4,128)} %copy-done.27) | copy-start | bytes 9220
  203.5 7.7 %copy-start.30 = (f32[3,256]{1,0:T(4,128)S(1)}, f32[3,256]{1,0:T(4,128)}, u32[]{:S(2)}) copy-start(f32[3,256]{1,0:T(4,128)} %copy-done.29) | copy-start | bytes 9220
  203.5 7.7 %copy-start.32 = (f32[3,256]{1,0:T(4,128)S(1)}, f32[3,256]{1,0:T(4,128)}, u32[]{:S(2)}) copy-start(f32[3,256]{1,0:T(4,128)} %copy-done.31) | copy-start | bytes 9220
  203.5 7.7 %copy-start.34 = (f32[3,1,256]{2,0,1:T(4,128)S(1)}, f32[3,1,256]{2,0,1:T(4,128)}, u32[]{:S(2)}) copy-start(f32[3,1,256]{2,0,1:T(4,128)} %copy-done.33) | copy-start | bytes 9220
  203.6 7.5 %collective-permute-start.3 = (f32[6,3,256]{2,0,1:T(8,128)S(1)}, f32[6,3,256]{2,0,1:T(8,128)S(1)}, u32[]{:S(2)}, u32[]{:S(2)}) collective-permute-start(f32[6,3,256]{2,0,1:T(8,128)S(1)} %slice.259), channel_id=1, source_target_pairs={{1,0},{2,1},{3,2},{4,3},{5,4},{6,5},{7,6},{9,8},{10,9},{11,10},{12... | collective-permute-start | bytes 55304 | tf_op jit(solution)/shard_map/ppermute | solution.py:86
  212.7 7.1 %copy-start.22 = (f32[4096]{0:T(1024)S(1)}, f32[4096]{0:T(1024)}, u32[]{:S(2)}) copy-start(f32[4096]{0:T(1024)} %copy-done.21) | copy-start | bytes 49156
  219.8 13.1 %copy-start.2 = (bf16[8,266,256]{2,1,0:T(8,128)(2,1)}, bf16[8,266,256]{2,1,0:T(8,128)(2,1)S(1)}, u32[]{:S(2)}) copy-start(bf16[8,266,256]{2,1,0:T(8,128)(2,1)S(1)} %all-to-all-done.3) | copy-start | bytes 3268612
  227.7 4.9 %copy-start.17 = (f32[128,256]{1,0:T(8,128)S(1)}, f32[128,256]{1,0:T(8,128)}, u32[]{:S(2)}) copy-start(f32[128,256]{1,0:T(8,128)} %param.16) | copy-start | bytes 393220
  227.7 4.9 %copy-start.19 = (f32[128,256]{1,0:T(8,128)S(1)}, f32[128,256]{1,0:T(8,128)}, u32[]{:S(2)}) copy-start(f32[128,256]{1,0:T(8,128)} %get-tuple-element.20) | copy-start | bytes 393220
  227.7 5.0 %copy-start.41 = (f32[256]{0:T(256)S(1)}, f32[256]{0:T(256)}, u32[]{:S(2)}) copy-start(f32[256]{0:T(256)} %copy-done.40) | copy-start | bytes 3076
  227.7 5.0 %copy-start.50 = (f32[128]{0:T(128)S(1)}, f32[128]{0:T(128)}, u32[]{:S(2)}) copy-start(f32[128]{0:T(128)} %copy-done.49) | copy-start | bytes 1540
  227.7 33.0 %all-to-all-start.4 = ((bf16[258,16,256]{2,0,1:T(8,128)(2,1)}), bf16[258,16,256]{2,0,1:T(8,128)(2,1)}, u32[]{:S(2)}, u32[]{:S(2)}) async-start(bf16[258,16,256]{2,0,1:T(8,128)(2,1)} %pad_maximum_fusion.2), calls=%async_computation.4 | async-start | bytes 4325376 | tf_op jit(solution)/shard_map/all_to_all | solution.py:229
  262.7 3.8 %copy-start.46 = (bf16[1024]{0:T(1024)(128)(2,1)S(1)}, bf16[1024]{0:T(1024)(128)(2,1)}, u32[]{:S(2)}) copy-start(bf16[1024]{0:T(1024)(128)(2,1)} %reshape.174) | copy-start | bytes 6148
  262.7 5.7 %copy-start.37 = (bf16[256,4]{0,1:T(4,128)(2,1)S(1)}, bf16[256,4]{0,1:T(4,128)(2,1)}, u32[]{:S(2)}) copy-start(bf16[256,4]{0,1:T(4,128)(2,1)} %param.19) | copy-start | bytes 6148
  262.7 5.7 %copy-start.47 = (f32[256]{0:T(256)S(1)}, f32[256]{0:T(256)}, u32[]{:S(2)}) copy-start(f32[256]{0:T(256)} %param.13) | copy-start | bytes 3076
  270.1 10.0 %copy-start.39 = (f32[512]{0:T(512)S(1)}, f32[512]{0:T(512)}, u32[]{:S(2)}) copy-start(f32[512]{0:T(512)} %copy-done.38) | copy-start | bytes 6148
  270.1 33.9 %all-to-all-start.5 = ((bf16[8,412,256]{2,1,0:T(8,128)(2,1)}), bf16[8,412,256]{2,1,0:T(8,128)(2,1)S(1)}, u32[]{:S(2)}, u32[]{:S(2)}) async-start(bf16[8,412,256]{2,1,0:T(8,128)(2,1)} %broadcast_in_dim.49), calls=%async_computation.5 | async-start | bytes 3407872 | tf_op jit(solution)/shard_map/all_to_all | solution.py:253
  278.0 6.1 %slice-start = ((bf16[8,266,256]{2,1,0:T(8,128)(2,1)}), bf16[8,256,256]{2,1,0:T(8,128)(2,1)S(1)}, s32[]{:S(2)}) async-start(bf16[8,266,256]{2,1,0:T(8,128)(2,1)} %copy-done.2), calls=%async_computation.9 | async-start | bytes 2097152 | tf_op jit(solution)/shard_map/slice | solution.py:260
  304.5 6.4 %copy-start.54 = (s32[64]{0:T(128)S(1)}, s32[64]{0:T(128)}, u32[]{:S(2)}) copy-start(s32[64]{0:T(128)} %iota_add_fusion) | copy-start | bytes 772
  305.7 6.6 %copy-start.5 = (bf16[16,256,256]{1,2,0:T(8,128)(2,1)S(1)}, bf16[16,256,256]{1,2,0:T(8,128)(2,1)}, u32[]{:S(2)}) copy-start(bf16[16,256,256]{1,2,0:T(8,128)(2,1)} %copy-done.4) | copy-start | bytes 6291460
  305.7 6.6 %copy-start.48 = (f32[512]{0:T(512)S(1)}, f32[512]{0:T(512)}, u32[]{:S(2)}) copy-start(f32[512]{0:T(512)} %dynamic-slice_reduce_fusion) | copy-start | bytes 6148
  (7 other events, 11.3 us)
Sparse Core Ops, SparseCore 0:
  11.1 56.1 all-gather.3
  101.8 55.8 all-gather.5
  212.8 87.0 all-gather.7

commit v3 on v2

--- a/solution.py
+++ b/solution.py
@@ -276,7 +276,12 @@
     gain_k = lax.dynamic_slice_in_dim(gain_full, k_ctx * f_cols, f_cols, 0)
     x0_k = jnp.dot(all_hot, embed_k, preferred_element_type=f32)
     u_k = (x0_k * r_all * gain_k[None, :]).astype(bf16)
-    d_w_in = jnp.einsum("td,jtc->jdc", u_k, dp_all, preferred_element_type=f32)
+    d_w_in = jnp.stack(
+        [
+            lax.dot_general(u_k, dp_all[j], (((0,), (0,)), ((), ())), preferred_element_type=f32)
+            for j in range(dp_all.shape[0])
+        ]
+    )
 
     v_rows = vocab // n_ctx
     own_hot = (ids_all[:, None] == (k_ctx * v_rows + jnp.arange(v_rows))[None, :]).astype(f32)

time: 331 us -> 328 us (level)
  local copies, waits for them, and re-layouts: 42.8 us -> 39.2 us
    unnamed x136 -> x139, local copies, waits for them, and re-layouts: 10.5 us -> 6.81 us
  transfers between devices with their start and end apart: 13 -> 13, of which waited for: 10 -> 10; matrix products, arithmetic and copies ran while one was open for 19% -> 20% of each run, Pallas kernels for 2% -> 2%
where the time goes in v3:
time: 328 us; the launch traced here: 326 us
  waiting for transfers between devices  142 us (43%)
  starting transfers between devices  52 us (16%)
  local copies, waits for them, and re-layouts  39.2 us (12%)
  matrix products  33.8 us (10%)
  other arithmetic  30.3 us (9%)
  between operations  16.9 us (5%)
  Pallas kernels  11.1 us (3%)
    all_to_all x1, waiting for transfers between devices, block(): lax.all_to_all(jnp.broadcast_to(embed[None, half:], (n_dp, vocab - half,...  31.2 us
    all_to_all x1, waiting for transfers between devices, block(): du_recv = lax.all_to_all(du_send, 'dp', 1, 1, tiled=True).astype(f32)  27.5 us
    all_to_all x1, waiting for transfers between devices, block(): w_out_cols = lax.all_to_all(w_out_later, 'dp', 1, 0, tiled=True)  26 us
    all_to_all x1, waiting for transfers between devices, block(): lax.all_to_all(jnp.broadcast_to(final[None], (n_ctx,) + final.shape), 'ct...  17.2 us
    all_gather x1, waiting for transfers between devices, block(): h_full = lax.all_gather(h, 'dp', axis=1, tiled=True)  15 us
    all_gather x1, waiting for transfers between devices, block(): packed_full = lax.all_gather(packed, 'dp', axis=1, tiled=True)  14.9 us
    ppermute x4, starting transfers between devices, shifted(): return lax.ppermute(block, axis, route)  13 us
    all_to_all x1, starting transfers between devices, block(): lax.all_to_all(jnp.broadcast_to(h_ids[None], (n_ctx,) + h_ids.shape), 'ct...  11.4 us
  transfers between devices with their start and end apart: 13, of which 10 were waited for; matrix products, arithmetic and copies ran while one was open for 20% of the time, Pallas kernels for 2%

profile of v3, /device:TPU:0, one launch (start us, length us, event | category | flops | bytes accessed | tf_op | source)
XLA Modules:
  0.0 325.7 jit_solution(17379746423411555852)
XLA Ops:
  9.0 1.0 fusion.68
  11.0 1.5 broadcast_in_dim.39
  12.5 5.7 %all-to-all-start = ((bf16[16,256,256]{2,1,0:T(8,128)(2,1)}), bf16[16,256,256]{2,1,0:T(8,128)(2,1)}, u32[]{:S(2)}, u32[]{:S(2)}) async-start(bf16[16,256,256]{2,1,0:T(8,128)(2,1)} %broadcast_in_dim.39), calls=%async_computation | async-start | bytes 4194304 | tf_op jit(solution)/shard_map/all_to_all | solution.py:138
  18.4 31.2 %all-to-all-done = bf16[16,256,256]{2,1,0:T(8,128)(2,1)} async-done(((bf16[16,256,256]{2,1,0:T(8,128)(2,1)}), bf16[16,256,256]{2,1,0:T(8,128)(2,1)}, u32[]{:S(2)}, u32[]{:S(2)}) %all-to-all-start) | async-done | bytes 2097184 | tf_op jit(solution)/shard_map/all_to_all | solution.py:138
  49.6 2.9 copy.85
  52.4 14.9 %all-gather.4.cloned.1.call-done = bf16[263,4096]{0,1:T(8,128)(2,1)} async-done(((bf16[263,256]{0,1:T(8,128)(2,1)}), bf16[263,4096]{0,1:T(8,128)(2,1)}) %all-gather.4.cloned.1.call-update) | async-done | bytes 2154512 | tf_op jit(solution)/shard_map/all_gather | solution.py:137
  67.4 1.7 slice.250
  69.1 1.0 multiply_reduce_fusion
  70.2 4.3 %fusion.1 = f32[256,4096]{1,0:T(8,128)S(1)} fusion(bf16[256,4096]{0,1:T(8,128)(2,1)} %bitcast.130, bf16[256,4096]{0,1:T(8,128)(2,1)S(1)} %slice.250, s32[256]{0:T(256)S(1)} %copy-done.44), kind=kOutput, calls=%fused_computation.14 | convolution fusion | flops 1082261504 | bytes 8389632 | tf_op jit(solution)/shard_map/dot_general | solution.py:156
  74.8 2.5 fusion.66
  77.3 1.9 fusion.8
  79.3 4.7 %collective-permute-start = (bf16[6,3,256]{2,0,1:T(8,128)(2,1)S(1)}, bf16[6,3,256]{2,0,1:T(8,128)(2,1)S(1)}, u32[]{:S(2)}, u32[]{:S(2)}) collective-permute-start(bf16[6,3,256]{2,0,1:T(8,128)(2,1)S(1)} %slice.254), channel_id=1, source_target_pairs={{0,1},{1,2},{2,3},{3,4},{4,5},{5,6},{6,7},{8,9},{9,10},{10,11},{11... | collective-permute-start | bytes 27656 | tf_op jit(solution)/shard_map/ppermute | solution.py:86
  84.1 1.3 collective-permute-done
  86.1 0.9 copy-done.8
  87.1 5.7 %collective-permute-start.1 = (bf16[127,256]{1,0:T(8,128)(2,1)S(1)}, bf16[127,256]{1,0:T(8,128)(2,1)S(1)}, u32[]{:S(2)}, u32[]{:S(2)}) collective-permute-start(bf16[127,256]{1,0:T(8,128)(2,1)S(1)} %slice.268), channel_id=1, source_target_pairs={{0,1},{1,2},{2,3},{3,4},{4,5},{5,6},{6,7},{8,9},{9,10},{10,11},{11... | collective-permute-start | bytes 195080 | tf_op jit(solution)/shard_map/ppermute | solution.py:86
  93.6 1.0 collective-permute-done.1
  94.7 0.9 maximum_convert_fusion.kv_ref
  95.5 4.4 %shard_map.177 = f32[256,256]{1,0:T(8,128)} custom-call(f32[384,256]{1,0:T(8,128)} %maximum_convert_fusion.kv_ref, f32[128,256]{1,0:T(8,128)} %fusion.50.g_ref), custom_call_target="tpu_custom_call" | custom-call | tf_op jit(solution)/shard_map/pallas_call | solution.py:27
  100.0 1.7 multiply_convert_fusion.2
  101.7 4.1 %copy.86 = bf16[256,4096]{0,1:T(8,128)(2,1)} copy(bf16[256,4096]{1,0:T(8,128)(2,1)} %param.18) | data formatting | bytes 4194304 | tf_op jit(solution)/shard_map/optimization_barrier | solution.py:142
  105.8 4.5 %all-to-all-start.1 = ((bf16[256,16,256]{0,2,1:T(8,128)(2,1)}), bf16[256,16,256]{0,2,1:T(8,128)(2,1)}, u32[]{:S(2)}, u32[]{:S(2)}) async-start(bf16[256,16,256]{0,2,1:T(8,128)(2,1)} %bitcast.132), calls=%async_computation.1 | async-start | bytes 4194304 | tf_op jit(solution)/shard_map/all_to_all | solution.py:143
  111.5 1.2 fusion.38
  112.7 26.0 %all-to-all-done.1 = bf16[256,16,256]{0,2,1:T(8,128)(2,1)} async-done(((bf16[256,16,256]{0,2,1:T(8,128)(2,1)}), bf16[256,16,256]{0,2,1:T(8,128)(2,1)}, u32[]{:S(2)}, u32[]{:S(2)}) %all-to-all-start.1) | async-done | bytes 2097184 | tf_op jit(solution)/shard_map/all_to_all | solution.py:143
  138.8 3.9 %copy.87 = bf16[16,256,256]{2,1,0:T(8,128)(2,1)} copy(bf16[16,256,256]{1,2,0:T(8,128)(2,1)} %bitcast.8) | data formatting | bytes 4194304 | tf_op jit(solution)/shard_map/all_to_all | solution.py:143
  142.7 15.0 %all-gather.6.cloned.1.call-done = bf16[256,4096]{1,0:T(8,128)(2,1)} async-done(((bf16[256,256]{1,0:T(8,128)(2,1)}), bf16[256,4096]{1,0:T(8,128)(2,1)}) %all-gather.6.cloned.1.call-update) | async-done | bytes 2097168 | tf_op jit(solution)/shard_map/all_gather | solution.py:175
  157.7 2.9 fusion.11
  161.5 4.3 %all-to-all-start.2 = ((f32[16,256,4]{1,2,0:T(4,128)}), f32[16,256,4]{1,2,0:T(4,128)}, u32[]{:S(2)}, u32[]{:S(2)}) async-start(f32[16,256,4]{1,2,0:T(4,128)} %broadcast_in_dim.43), calls=%async_computation.2 | async-start | bytes 131072 | tf_op jit(solution)/shard_map/all_to_all | solution.py:181
  166.4 1.3 slice.269
  167.7 1.7 dynamic-slice_reduce_fusion
  169.4 2.4 all-to-all-done.2
  171.8 0.9 reduce_sum.184
  174.9 0.8 copy.88
  175.7 2.2 convolution_convert_fusion
  177.9 1.7 multiply_bitcast_fusion.2
  180.6 1.3 collective-permute-start.2
  182.1 1.1 broadcast_in_dim.45
  183.2 11.4 %all-to-all-start.3 = ((bf16[8,266,256]{2,1,0:T(8,128)(2,1)}), bf16[8,266,256]{2,1,0:T(8,128)(2,1)S(1)}, u32[]{:S(2)}, u32[]{:S(2)}) async-start(bf16[8,266,256]{2,1,0:T(8,128)(2,1)} %broadcast_in_dim.45), calls=%async_computation.3 | async-start | bytes 2228224 | tf_op jit(solution)/shard_map/all_to_all | solution.py:192
  194.7 0.9 maximum_maximum_fusion.dm_ref
  195.6 6.7 %shard_map.178 = (f32[256,256]{1,0:T(8,128)}, f32[128,256]{1,0:T(8,128)}) custom-call(f32[384,256]{1,0:T(8,128)} %maximum_maximum_fusion.dm_ref, f32[384,256]{1,0:T(8,128)} %maximum_convert_fusion.kv_ref, f32[128,256]{1,0:T(8,128)} %fusion.50.g_ref), custom_call_target="tpu_custom_call" | custom-call | tf_op jit(solution)/shard_map/pallas_call | solution.py:64
  202.3 1.0 multiply_bitcast_fusion.1
  204.2 1.3 collective-permute-start.3
  205.5 5.9 %collective-permute-done.3 = f32[6,3,256]{2,0,1:T(8,128)S(1)} collective-permute-done((f32[6,3,256]{2,0,1:T(8,128)S(1)}, f32[6,3,256]{2,0,1:T(8,128)S(1)}, u32[]{:S(2)}, u32[]{:S(2)}) %collective-permute-start.3) | collective-permute-done | bytes 18464 | tf_op jit(solution)/shard_map/ppermute | solution.py:86
  211.5 1.4 fusion.95
  213.0 7.1 %convolution_bitcast_fusion = f32[256,4096]{1,0:T(8,128)} fusion(bf16[3,4096,256]{2,1,0:T(8,128)(2,1)} %param.14, f32[262,3,256]{2,0,1:T(8,128)S(1)} %pad_maximum_fusion.4, f32[3,256]{1,0:T(4,128)S(1)} %copy-done.30, f32[3,256]{1,0:T(4,128)S(1)} %copy-done.32, f32[3,256]{1,0:T(4,128)S(1)} %get-tuple-element.139, f32[3,256]{1,0:T(4,128)S(1)} %get-tuple-element.140, ...), kind=kOutput, calls=%fused_computation.1 | convolution fusion | flops 1613758464 | bytes 16019456 | tf_op jit(solution)/shard_map/tjc,jdc->td/dot_general | solution.py:217
  220.1 6.1 %fusion.67 = (bf16[256,4096]{1,0:T(8,128)(2,1)S(1)}, f32[256]{0:T(256)S(1)}) fusion(f32[256,4096]{1,0:T(8,128)} %convolution_bitcast_fusion, f32[256,4096]{1,0:T(8,128)} %copy-done.10, f32[4096]{0:T(1024)S(1)} %copy-done.22), kind=kLoop, calls=%fused_computation.185 | loop fusion | flops 4194048 | bytes 10503168 | tf_op jit(solution)/shard_map/convert_element_type | solution.py:224
  226.4 1.5 pad_maximum_fusion.2
  227.9 4.8 %all-to-all-start.4 = ((bf16[258,16,256]{2,0,1:T(8,128)(2,1)}), bf16[258,16,256]{2,0,1:T(8,128)(2,1)}, u32[]{:S(2)}, u32[]{:S(2)}) async-start(bf16[258,16,256]{2,0,1:T(8,128)(2,1)} %pad_maximum_fusion.2), calls=%async_computation.4 | async-start | bytes 4325376 | tf_op jit(solution)/shard_map/all_to_all | solution.py:229
  233.5 27.5 %all-to-all-done.4 = bf16[258,16,256]{2,0,1:T(8,128)(2,1)} async-done(((bf16[258,16,256]{2,0,1:T(8,128)(2,1)}), bf16[258,16,256]{2,0,1:T(8,128)(2,1)}, u32[]{:S(2)}, u32[]{:S(2)}) %all-to-all-start.4) | async-done | bytes 2113568 | tf_op jit(solution)/shard_map/all_to_all | solution.py:229
  260.9 1.9 convert_element_type.196
  263.2 1.7 copy-done.1
  267.7 0.9 slice_reduce_fusion.1
  269.0 1.3 broadcast_in_dim.49
  270.3 8.1 %all-to-all-start.5 = ((bf16[8,412,256]{2,1,0:T(8,128)(2,1)}), bf16[8,412,256]{2,1,0:T(8,128)(2,1)}, u32[]{:S(2)}, u32[]{:S(2)}) async-start(bf16[8,412,256]{2,1,0:T(8,128)(2,1)} %broadcast_in_dim.49), calls=%async_computation.5 | async-start | bytes 3407872 | tf_op jit(solution)/shard_map/all_to_all | solution.py:253
  278.5 1.1 reshape.181
  279.6 0.9 select_reduce_fusion
  280.6 2.7 convolution_convert_fusion.1
  283.4 2.6 multiply_convert_fusion
  285.9 1.5 fusion.72
  287.4 17.2 %all-to-all-done.5 = bf16[8,412,256]{2,1,0:T(8,128)(2,1)} async-done(((bf16[8,412,256]{2,1,0:T(8,128)(2,1)}), bf16[8,412,256]{2,1,0:T(8,128)(2,1)}, u32[]{:S(2)}, u32[]{:S(2)}) %all-to-all-start.5) | async-done | bytes 1687584 | tf_op jit(solution)/shard_map/all_to_all | solution.py:253
  304.6 1.1 slice.282
  309.9 1.3 slice.289
  311.7 1.4 fusion.13
  313.1 2.1 convolution_bitcast_fusion.1
  316.8 1.2 pad_maximum_fusion.3
  (223 shorter events, 21.5 us)
Async XLA Ops:
  7.2 60.2 %all-gather.4.cloned.1.call-start = ((), (), s32[]{:S(2)}) async-start(), calls=%async_computation.6 | async-start | bytes 3342336 | tf_op jit(solution)/shard_map/all_gather | solution.py:137
  12.5 5.8 %copy-start.35 = (f32[3,7,256]{2,1,0:T(8,128)S(1)}, f32[3,7,256]{2,1,0:T(8,128)}, u32[]{:S(2)}) copy-start(f32[3,7,256]{2,1,0:T(8,128)} %param.15) | copy-start | bytes 64516
  12.5 37.0 %all-to-all-start = ((bf16[16,256,256]{2,1,0:T(8,128)(2,1)}), bf16[16,256,256]{2,1,0:T(8,128)(2,1)}, u32[]{:S(2)}, u32[]{:S(2)}) async-start(bf16[16,256,256]{2,1,0:T(8,128)(2,1)} %broadcast_in_dim.39), calls=%async_computation | async-start | bytes 4194304 | tf_op jit(solution)/shard_map/all_to_all | solution.py:138
  18.2 139.5 %all-gather.6.cloned.1.call-start = ((), (), s32[]{:S(2)}) async-start(), calls=%async_computation.7 | async-start | bytes 2228224 | tf_op jit(solution)/shard_map/all_gather | solution.py:175
  18.4 67.1 %copy-start.25 = (f32[3,256]{1,0:T(4,128)}, f32[3,256]{1,0:T(4,128)S(1)}, u32[]{:S(2)}) copy-start(f32[3,256]{1,0:T(4,128)S(1)} %get-tuple-element.141) | copy-start | bytes 9220
  18.4 67.1 %copy-start.27 = (f32[3,256]{1,0:T(4,128)}, f32[3,256]{1,0:T(4,128)S(1)}, u32[]{:S(2)}) copy-start(f32[3,256]{1,0:T(4,128)S(1)} %get-tuple-element.142) | copy-start | bytes 9220
  18.4 67.0 %copy-start.29 = (f32[3,256]{1,0:T(4,128)}, f32[3,256]{1,0:T(4,128)S(1)}, u32[]{:S(2)}) copy-start(f32[3,256]{1,0:T(4,128)S(1)} %get-tuple-element.137) | copy-start | bytes 9220
  18.4 67.0 %copy-start.31 = (f32[3,256]{1,0:T(4,128)}, f32[3,256]{1,0:T(4,128)S(1)}, u32[]{:S(2)}) copy-start(f32[3,256]{1,0:T(4,128)S(1)} %get-tuple-element.138) | copy-start | bytes 9220
  52.4 17.7 %copy-start.4 = (bf16[16,256,256]{1,2,0:T(8,128)(2,1)}, bf16[16,256,256]{1,2,0:T(8,128)(2,1)S(1)}, u32[]{:S(2)}) copy-start(bf16[16,256,256]{1,2,0:T(8,128)(2,1)S(1)} %copy.85) | copy-start | bytes 6291460
  69.1 5.4 %copy-start.6 = (bf16[256,4096]{0,1:T(8,128)(2,1)}, bf16[256,4096]{0,1:T(8,128)(2,1)S(1)}, u32[]{:S(2)}) copy-start(bf16[256,4096]{0,1:T(8,128)(2,1)S(1)} %slice.250) | copy-start | bytes 6291460
  69.1 8.2 %slice-start.1 = ((s8[6291456]{0:T(1024)(128)(4,1)}), s8[4194304]{0:T(1024)(128)(4,1)S(1)}, s32[]{:S(2)}) async-start(s8[6291456]{0:T(1024)(128)(4,1)} %bitcast.150), calls=%async_computation.10 | async-start | bytes 8388608
  70.2 4.3 %copy-start.38 = (f32[512]{0:T(512)}, f32[512]{0:T(512)S(1)}, u32[]{:S(2)}) copy-start(f32[512]{0:T(512)S(1)} %add_rsqrt_fusion) | copy-start | bytes 6148
  70.2 4.5 %copy-start = (bf16[263,4096]{0,1:T(8,128)(2,1)S(1)}, bf16[263,4096]{0,1:T(8,128)(2,1)}, u32[]{:S(2)}) copy-start(bf16[263,4096]{0,1:T(8,128)(2,1)} %all-gather.4.cloned.1.call-done) | copy-start | bytes 6463492
  70.2 7.1 %slice-start.2 = ((s8[6291456]{0:T(1024)(128)(4,1)}), s8[2097152]{0:T(1024)(128)(4,1)S(1)}, s32[]{:S(2)}) async-start(s8[6291456]{0:T(1024)(128)(4,1)} %bitcast.150), calls=%async_computation.11 | async-start | bytes 4194304
  74.5 2.8 copy-start.10
  74.7 2.5 copy-start.42
  77.3 6.7 %copy-start.53 = (f32[256]{0:T(256)S(1)}, f32[256]{0:T(256)}, u32[]{:S(2)}) copy-start(f32[256]{0:T(256)} %param.17) | copy-start | bytes 3076
  77.3 15.5 %copy-start.16 = (f32[128,256]{1,0:T(8,128)S(1)}, f32[128,256]{1,0:T(8,128)}, u32[]{:S(2)}) copy-start(f32[128,256]{1,0:T(8,128)} %param.16) | copy-start | bytes 393220
  79.2 7.8 %copy-start.12 = (bf16[256,3,256]{2,0,1:T(8,128)(2,1)}, bf16[256,3,256]{2,0,1:T(8,128)(2,1)S(1)}, u32[]{:S(2)}) copy-start(bf16[256,3,256]{2,0,1:T(8,128)(2,1)S(1)} %fusion.8) | copy-start | bytes 1179652
  79.3 6.1 %collective-permute-start = (bf16[6,3,256]{2,0,1:T(8,128)(2,1)S(1)}, bf16[6,3,256]{2,0,1:T(8,128)(2,1)S(1)}, u32[]{:S(2)}, u32[]{:S(2)}) collective-permute-start(bf16[6,3,256]{2,0,1:T(8,128)(2,1)S(1)} %slice.254), channel_id=1, source_target_pairs={{0,1},{1,2},{2,3},{3,4},{4,5},{5,6},{6,7},{8,9},{9,10},{10,11},{11... | collective-permute-start | bytes 27656 | tf_op jit(solution)/shard_map/ppermute | solution.py:86
  84.0 17.6 %copy-start.49 = (f32[128]{0:T(128)}, f32[128]{0:T(128)S(1)}, u32[]{:S(2)}) copy-start(f32[128]{0:T(128)S(1)} %iota_convert_fusion) | copy-start | bytes 1540
  84.1 17.6 %copy-start.40 = (f32[256]{0:T(256)}, f32[256]{0:T(256)S(1)}, u32[]{:S(2)}) copy-start(f32[256]{0:T(256)S(1)} %neg.7) | copy-start | bytes 3076
  84.1 17.6 %copy-start.33 = (f32[3,1,256]{2,0,1:T(4,128)}, f32[3,1,256]{2,0,1:T(4,128)S(1)}, u32[]{:S(2)}) copy-start(f32[3,1,256]{2,0,1:T(4,128)S(1)} %copy.116) | copy-start | bytes 9220
  85.4 9.3 %copy-start.23 = (bf16[6,3,256]{2,0,1:T(8,128)(2,1)}, bf16[6,3,256]{2,0,1:T(8,128)(2,1)S(1)}, u32[]{:S(2)}) copy-start(bf16[6,3,256]{2,0,1:T(8,128)(2,1)S(1)} %collective-permute-done) | copy-start | bytes 27652
  87.1 7.6 %collective-permute-start.1 = (bf16[127,256]{1,0:T(8,128)(2,1)S(1)}, bf16[127,256]{1,0:T(8,128)(2,1)S(1)}, u32[]{:S(2)}, u32[]{:S(2)}) collective-permute-start(bf16[127,256]{1,0:T(8,128)(2,1)S(1)} %slice.268), channel_id=1, source_target_pairs={{0,1},{1,2},{2,3},{3,4},{4,5},{5,6},{6,7},{8,9},{9,10},{10,11},{11... | collective-permute-start | bytes 195080 | tf_op jit(solution)/shard_map/ppermute | solution.py:86
  105.8 33.0 %all-to-all-start.1 = ((bf16[256,16,256]{0,2,1:T(8,128)(2,1)}), bf16[256,16,256]{0,2,1:T(8,128)(2,1)}, u32[]{:S(2)}, u32[]{:S(2)}) async-start(bf16[256,16,256]{0,2,1:T(8,128)(2,1)} %bitcast.132), calls=%async_computation.1 | async-start | bytes 4194304 | tf_op jit(solution)/shard_map/all_to_all | solution.py:143
  157.7 3.0 copy-start.36
  160.7 17.2 %copy-start.14 = (bf16[256,256]{1,0:T(8,128)(2,1)}, bf16[256,256]{1,0:T(8,128)(2,1)S(1)}, u32[]{:S(2)}) copy-start(bf16[256,256]{1,0:T(8,128)(2,1)S(1)} %fusion.11) | copy-start | bytes 393220
  161.5 10.3 %all-to-all-start.2 = ((f32[16,256,4]{1,2,0:T(4,128)}), f32[16,256,4]{1,2,0:T(4,128)}, u32[]{:S(2)}, u32[]{:S(2)}) async-start(f32[16,256,4]{1,2,0:T(4,128)} %broadcast_in_dim.43), calls=%async_computation.2 | async-start | bytes 131072 | tf_op jit(solution)/shard_map/all_to_all | solution.py:181
  177.9 4.0 %copy-start.18 = (f32[256,4]{1,0:T(8,128)S(1)}, f32[256,4]{1,0:T(8,128)}, u32[]{:S(2)}) copy-start(f32[256,4]{1,0:T(8,128)} %copy.88) | copy-start | bytes 12292
  177.9 4.1 %copy-start.51 = (bf16[256]{0:T(256)(128)(2,1)S(1)}, bf16[256]{0:T(256)(128)(2,1)}, u32[]{:S(2)}) copy-start(bf16[256]{0:T(256)(128)(2,1)} %get-tuple-element.132) | copy-start | bytes 1540
  177.9 4.1 %copy-start.52 = (bf16[256]{0:T(256)(128)(2,1)S(1)}, bf16[256]{0:T(256)(128)(2,1)}, u32[]{:S(2)}) copy-start(bf16[256]{0:T(256)(128)(2,1)} %get-tuple-element.133) | copy-start | bytes 1540
  177.9 4.1 %copy-start.15 = (bf16[256,256]{1,0:T(8,128)(2,1)S(1)}, bf16[256,256]{1,0:T(8,128)(2,1)}, u32[]{:S(2)}) copy-start(bf16[256,256]{1,0:T(8,128)(2,1)} %multiply_convert_fusion.2) | copy-start | bytes 393220
  179.8 14.8 %copy-start.45 = (f32[384]{0:T(512)S(1)}, f32[384]{0:T(512)}, u32[]{:S(2)}) copy-start(f32[384]{0:T(512)} %pad.29.clone) | copy-start | bytes 4612
  180.6 14.0 %collective-permute-start.2 = (bf16[127,256]{1,0:T(8,128)(2,1)S(1)}, bf16[127,256]{1,0:T(8,128)(2,1)S(1)}, u32[]{:S(2)}, u32[]{:S(2)}) collective-permute-start(bf16[127,256]{1,0:T(8,128)(2,1)S(1)} %slice.436), channel_id=1, source_target_pairs={{1,0},{2,1},{3,2},{4,3},{5,4},{6,5},{7,6},{9,8},{10,9},{11,10},{12... | collective-permute-start | bytes 195080 | tf_op jit(solution)/shard_map/ppermute | solution.py:86
  183.2 19.1 %copy-start.9 = (f32[256,3,256]{2,0,1:T(8,128)S(1)}, f32[256,3,256]{2,0,1:T(8,128)}, u32[]{:S(2)}) copy-start(f32[256,3,256]{2,0,1:T(8,128)} %copy-done.8) | copy-start | bytes 2359300
  183.2 36.9 %all-to-all-start.3 = ((bf16[8,266,256]{2,1,0:T(8,128)(2,1)}), bf16[8,266,256]{2,1,0:T(8,128)(2,1)S(1)}, u32[]{:S(2)}, u32[]{:S(2)}) async-start(bf16[8,266,256]{2,1,0:T(8,128)(2,1)} %broadcast_in_dim.45), calls=%async_computation.3 | async-start | bytes 2228224 | tf_op jit(solution)/shard_map/all_to_all | solution.py:192
  194.6 118.5 %all-gather.8.cloned.1.call-start = ((), (), s32[]{:S(2)}) async-start(), calls=%async_computation.8 | async-start | bytes 3538944 | tf_op jit(solution)/shard_map/all_gather | solution.py:216
  194.7 8.7 %copy-start.13 = (bf16[256,3,256]{2,0,1:T(8,128)(2,1)S(1)}, bf16[256,3,256]{2,0,1:T(8,128)(2,1)}, u32[]{:S(2)}) copy-start(bf16[256,3,256]{2,0,1:T(8,128)(2,1)} %copy-done.12) | copy-start | bytes 1179652
  194.7 8.7 %copy-start.24 = (bf16[6,3,256]{2,0,1:T(8,128)(2,1)S(1)}, bf16[6,3,256]{2,0,1:T(8,128)(2,1)}, u32[]{:S(2)}) copy-start(bf16[6,3,256]{2,0,1:T(8,128)(2,1)} %copy-done.23) | copy-start | bytes 27652
  203.3 8.2 %copy-start.26 = (f32[3,256]{1,0:T(4,128)S(1)}, f32[3,256]{1,0:T(4,128)}, u32[]{:S(2)}) copy-start(f32[3,256]{1,0:T(4,128)} %copy-done.25) | copy-start | bytes 9220
  203.3 8.2 %copy-start.28 = (f32[3,256]{1,0:T(4,128)S(1)}, f32[3,256]{1,0:T(4,128)}, u32[]{:S(2)}) copy-start(f32[3,256]{1,0:T(4,128)} %copy-done.27) | copy-start | bytes 9220
  203.3 8.2 %copy-start.30 = (f32[3,256]{1,0:T(4,128)S(1)}, f32[3,256]{1,0:T(4,128)}, u32[]{:S(2)}) copy-start(f32[3,256]{1,0:T(4,128)} %copy-done.29) | copy-start | bytes 9220
  203.3 8.2 %copy-start.32 = (f32[3,256]{1,0:T(4,128)S(1)}, f32[3,256]{1,0:T(4,128)}, u32[]{:S(2)}) copy-start(f32[3,256]{1,0:T(4,128)} %copy-done.31) | copy-start | bytes 9220
  203.3 8.2 %copy-start.34 = (f32[3,1,256]{2,0,1:T(4,128)S(1)}, f32[3,1,256]{2,0,1:T(4,128)}, u32[]{:S(2)}) copy-start(f32[3,1,256]{2,0,1:T(4,128)} %copy-done.33) | copy-start | bytes 9220
  204.2 7.2 %collective-permute-start.3 = (f32[6,3,256]{2,0,1:T(8,128)S(1)}, f32[6,3,256]{2,0,1:T(8,128)S(1)}, u32[]{:S(2)}, u32[]{:S(2)}) collective-permute-start(f32[6,3,256]{2,0,1:T(8,128)S(1)} %slice.271), channel_id=1, source_target_pairs={{1,0},{2,1},{3,2},{4,3},{5,4},{6,5},{7,6},{9,8},{10,9},{11,10},{12... | collective-permute-start | bytes 55304 | tf_op jit(solution)/shard_map/ppermute | solution.py:86
  213.0 7.1 %copy-start.22 = (f32[4096]{0:T(1024)S(1)}, f32[4096]{0:T(1024)}, u32[]{:S(2)}) copy-start(f32[4096]{0:T(1024)} %copy-done.21) | copy-start | bytes 49156
  220.1 58.4 %copy-start.2 = (bf16[8,266,256]{2,1,0:T(8,128)(2,1)}, bf16[8,266,256]{2,1,0:T(8,128)(2,1)S(1)}, u32[]{:S(2)}) copy-start(bf16[8,266,256]{2,1,0:T(8,128)(2,1)S(1)} %all-to-all-done.3) | copy-start | bytes 3268612
  227.9 4.9 %copy-start.17 = (f32[128,256]{1,0:T(8,128)S(1)}, f32[128,256]{1,0:T(8,128)}, u32[]{:S(2)}) copy-start(f32[128,256]{1,0:T(8,128)} %param.16) | copy-start | bytes 393220
  227.9 4.9 %copy-start.19 = (f32[128,256]{1,0:T(8,128)S(1)}, f32[128,256]{1,0:T(8,128)}, u32[]{:S(2)}) copy-start(f32[128,256]{1,0:T(8,128)} %get-tuple-element.20) | copy-start | bytes 393220
  227.9 4.9 %copy-start.41 = (f32[256]{0:T(256)S(1)}, f32[256]{0:T(256)}, u32[]{:S(2)}) copy-start(f32[256]{0:T(256)} %copy-done.40) | copy-start | bytes 3076
  227.9 4.9 %copy-start.50 = (f32[128]{0:T(128)S(1)}, f32[128]{0:T(128)}, u32[]{:S(2)}) copy-start(f32[128]{0:T(128)} %copy-done.49) | copy-start | bytes 1540
  227.9 33.0 %all-to-all-start.4 = ((bf16[258,16,256]{2,0,1:T(8,128)(2,1)}), bf16[258,16,256]{2,0,1:T(8,128)(2,1)}, u32[]{:S(2)}, u32[]{:S(2)}) async-start(bf16[258,16,256]{2,0,1:T(8,128)(2,1)} %pad_maximum_fusion.2), calls=%async_computation.4 | async-start | bytes 4325376 | tf_op jit(solution)/shard_map/all_to_all | solution.py:229
  262.9 3.7 %copy-start.46 = (bf16[1024]{0:T(1024)(128)(2,1)S(1)}, bf16[1024]{0:T(1024)(128)(2,1)}, u32[]{:S(2)}) copy-start(bf16[1024]{0:T(1024)(128)(2,1)} %reshape.174) | copy-start | bytes 6148
  262.9 5.7 %copy-start.37 = (bf16[256,4]{0,1:T(4,128)(2,1)S(1)}, bf16[256,4]{0,1:T(4,128)(2,1)}, u32[]{:S(2)}) copy-start(bf16[256,4]{0,1:T(4,128)(2,1)} %param.19) | copy-start | bytes 6148
  262.9 5.7 %copy-start.47 = (f32[256]{0:T(256)S(1)}, f32[256]{0:T(256)}, u32[]{:S(2)}) copy-start(f32[256]{0:T(256)} %param.13) | copy-start | bytes 3076
  270.3 34.3 %all-to-all-start.5 = ((bf16[8,412,256]{2,1,0:T(8,128)(2,1)}), bf16[8,412,256]{2,1,0:T(8,128)(2,1)}, u32[]{:S(2)}, u32[]{:S(2)}) async-start(bf16[8,412,256]{2,1,0:T(8,128)(2,1)} %broadcast_in_dim.49), calls=%async_computation.5 | async-start | bytes 3407872 | tf_op jit(solution)/shard_map/all_to_all | solution.py:253
  278.5 4.8 %copy-start.5 = (bf16[16,256,256]{1,2,0:T(8,128)(2,1)S(1)}, bf16[16,256,256]{1,2,0:T(8,128)(2,1)}, u32[]{:S(2)}) copy-start(bf16[16,256,256]{1,2,0:T(8,128)(2,1)} %copy-done.4) | copy-start | bytes 6291460
  278.5 4.8 %copy-start.48 = (f32[512]{0:T(512)S(1)}, f32[512]{0:T(512)}, u32[]{:S(2)}) copy-start(f32[512]{0:T(512)} %dynamic-slice_reduce_fusion) | copy-start | bytes 6148
  279.6 3.7 %copy-start.7 = (bf16[256,4096]{0,1:T(8,128)(2,1)S(1)}, bf16[256,4096]{0,1:T(8,128)(2,1)}, u32[]{:S(2)}) copy-start(bf16[256,4096]{0,1:T(8,128)(2,1)} %copy-done.6) | copy-start | bytes 6291460
  283.3 2.6 slice-start
  306.1 5.6 %copy-start.54 = (s32[64]{0:T(128)S(1)}, s32[64]{0:T(128)}, u32[]{:S(2)}) copy-start(s32[64]{0:T(128)} %iota_add_fusion) | copy-start | bytes 772
  306.5 6.6 %copy-start.56 = (bf16[2048,512]{1,0:T(8,128)(2,1)S(1)}, bf16[2048,512]{1,0:T(8,128)(2,1)}, u32[]{:S(2)}) copy-start(bf16[2048,512]{1,0:T(8,128)(2,1)} %multiply_convert_fusion) | copy-start | bytes 6291460
  313.1 2.2 copy-start.55
  (9 other events, 15.6 us)
Sparse Core Ops, SparseCore 0:
  11.1 56.2 all-gather.3
  101.8 55.8 all-gather.5
  213.1 87.3 all-gather.7
